TPU v7x, 32 devices: a whole 2x2x4 slice. The times are simulated.
32 devices in a mesh: groups: 2 (over y), space: 4 (over z), tm: 2 (over x), heads: 2 (over core).
Axes of the slice: x: 2, y: 2, z: 4, core: 2. Of those that a mesh axis runs over, the one named last changes fastest.
Arguments:
- latent: bfloat16 [12, 16, 52, 1536], P(('groups', 'tm'), 'space', None, 'heads'), parts along dimension 0, may hold values from -6 to 6
- query_weight: bfloat16 [1536, 1536], P(None, 'heads'), may hold values from -0.15625 to 0.15625
- key_weight: bfloat16 [1536, 1536], P(None, 'heads'), may hold values from -0.15625 to 0.15625
- value_weight: bfloat16 [1536, 1536], P(None, 'heads'), may hold values from -0.15625 to 0.15625
- output_weight: bfloat16 [1536, 1536], P('heads'), may hold values from -0.15625 to 0.15625
- query_gain: float32 [1536], P('heads'), may hold values from 0.6 to 7
- key_gain: float32 [1536], P('heads'), may hold values from 0.6 to 7
- modulation: float32 [16, 3, 1536], replicated, may hold values from -4 to 4
- noise_level: int32 [4], P(('groups', 'tm')), parts along dimension 0, may hold values from 0 to 15
- tile_pattern: int32 [4, 3, 6, 3], P('space'), may hold values from 0 to 1, as said below
Outputs:
- updated: bfloat16 [12, 16, 52, 1536], P(('groups', 'tm'), 'space', None, 'heads'), parts along dimension 0
There are 2 independent parts, one for each index of `groups`. A program takes and returns all parts, laid end to end along the dimension named above; an argument that names none is the same for every part. Nothing has to cross between parts.
Inputs may be any that keep to these rules, and one draw needn't show every extreme that they name: tile_pattern[s, f, 3 + f, 1] is 1 for every strip s and frame f; entries that name a strip outside the grid are 0.
All inputs are finite; a program needn't handle non-finite values.
Results may differ from a plain program's by a relative error of at most 0.0045.
The roundings to bfloat16 on the way count: a program that leaves them out, or rounds other values in their place, can miss the bound.
Values may be sent and summed in bfloat16 or wider, within the bound.
No kernel may reach another device: no remote copies, remote signals or barrier semaphores. Data moves between devices by JAX's collectives and lax.ppermute only.
A program may use at most 128 MiB of HBM per device.

v0:
```python
import functools
import math

import jax
import jax.numpy as jnp
from jax import lax
from jax.experimental import pallas as pl
from jax.experimental.pallas import tpu as pltpu
from jax.sharding import PartitionSpec as P

HD = 128


EPSILON = 1e-06


def from_behind(value, axis, steps):
    count = lax.axis_size(axis)
    first, last = (max(0, -steps), min(count, count - steps))
    return lax.ppermute(value, axis, [(source, source + steps) for source in range(first, last)])


def gather_heads(half):
    if lax.axis_size("heads") != 2:
        return lax.all_gather(half, "heads", axis=half.ndim - 1, tiled=True)
    me = lax.axis_index("heads")
    other = lax.ppermute(half, "heads", [(0, 1), (1, 0)])
    first = jnp.where(me == 0, half, other)
    second = jnp.where(me == 0, other, half)
    return jnp.concatenate([first, second], axis=-1)


def sum_heads(partial, local_width):
    if lax.axis_size("heads") != 2:
        return lax.psum_scatter(partial, "heads", scatter_dimension=1, tiled=True)
    me = lax.axis_index("heads")
    mine = lax.dynamic_slice_in_dim(partial, me * local_width, local_width, 1)
    theirs = lax.dynamic_slice_in_dim(partial, (1 - me) * local_width, local_width, 1)
    return mine + lax.ppermute(theirs, "heads", [(0, 1), (1, 0)])


def sum_pair(value):
    if lax.axis_size("heads") != 2:
        return lax.psum(value, "heads")
    return value + lax.ppermute(value, "heads", [(0, 1), (1, 0)])


def output_columns(attended, output_weight, local_width):
    if lax.axis_size("heads") != 2:
        partial = jnp.dot(attended, output_weight, preferred_element_type=jnp.float32)
        return sum_heads(partial, local_width)
    me = lax.axis_index("heads")
    swap = [(0, 1), (1, 0)]
    mine = lax.dynamic_slice_in_dim(output_weight, me * local_width, local_width, 1)
    theirs = lax.dynamic_slice_in_dim(output_weight, (1 - me) * local_width, local_width, 1)
    received = lax.ppermute(theirs, "heads", swap)
    other = lax.ppermute(attended, "heads", swap)
    return jnp.dot(attended, mine, preferred_element_type=jnp.float32) + jnp.dot(
        other, received, preferred_element_type=jnp.float32
    )


GROUP = 3


def attention_kernel(score_scale, n_tiles, group_size, has_in, has_out, order_ref, count_ref, q_ref, *refs):
    kv_ref = refs[0]
    carry_in = refs[1:4] if has_in else ()
    outs = refs[1 + len(carry_in) : -4]
    s_scr, m_scr, l_scr, acc_scr = refs[-4:]
    frame = pl.program_id(1)
    count = count_ref[frame]
    q = q_ref[...]
    groups = [list(range(i, min(i + group_size, n_tiles))) for i in range(0, n_tiles, group_size)]
    m_scr[...] = jnp.full(m_scr.shape, -jnp.inf, jnp.float32)
    for group in groups:

        @pl.when(count > group[0])
        def _():
            for n in group:
                s = (
                    lax.dot_general(
                        q, kv_ref[0, order_ref[frame, n]], (((1,), (1,)), ((), ())),
                        preferred_element_type=jnp.float32,
                    )
                    * score_scale
                )
                s = jnp.where(n < count, s, -jnp.inf)
                s_scr[n] = s
                m_scr[...] = jnp.maximum(m_scr[...], s)

    m = jnp.max(m_scr[...], axis=1, keepdims=True)
    if has_in:
        acc_in, m_in, l_in = carry_in
        m_prev = m_in[:, 0:1]
        m = jnp.maximum(m_prev, m)
        rescale = jnp.exp(m_prev - m)
        acc_scr[...] = acc_in[...] * rescale
    else:
        acc_scr[...] = jnp.zeros(acc_scr.shape, jnp.float32)
    l_scr[...] = jnp.zeros(l_scr.shape, jnp.float32)
    for group in groups:

        @pl.when(count > group[0])
        def _():
            for n in group:
                e = jnp.exp(s_scr[n] - m)
                l_scr[...] += e
                acc_scr[...] += jnp.dot(
                    e.astype(jnp.bfloat16), kv_ref[1, order_ref[frame, n]],
                    preferred_element_type=jnp.float32,
                )

    total = jnp.sum(l_scr[...], axis=1, keepdims=True)
    if has_in:
        total = l_in[:, 0:1] * rescale + total
    if has_out:
        acc_out, m_out, l_out = outs
        acc_out[...] = acc_scr[...]
        m_out[...] = jnp.broadcast_to(m, m_out.shape)
        l_out[...] = jnp.broadcast_to(total, l_out.shape)
    else:
        outs[0][...] = (acc_scr[...] / total).astype(outs[0].dtype)


def attention(visible, queries, kv_list, frames, tile_size, carry=None, last=True):
    local_width = queries.shape[1]
    heads = local_width // HD
    slots = [t for _, ids in kv_list for t in ids]
    n_tiles = len(slots)
    kv_all = jnp.concatenate([kv for kv, _ in kv_list], axis=1)
    seen = visible[:, jnp.array(slots, jnp.int32)]
    order = jnp.argsort(1 - seen, axis=1, stable=True).astype(jnp.int32)
    count = jnp.sum(seen, axis=1).astype(jnp.int32)
    has_in = carry is not None
    group_size = n_tiles if n_tiles >= 4 * GROUP else GROUP
    kernel = functools.partial(
        attention_kernel, 1.0 / math.sqrt(HD), n_tiles, group_size, has_in, not last
    )
    kv_spec = pl.BlockSpec((2, n_tiles, tile_size, HD), lambda h, f, o, c: (0, 0, 0, h))
    row_spec = pl.BlockSpec((tile_size, HD), lambda h, f, o, c: (f, h))
    row_f32 = jax.ShapeDtypeStruct(queries.shape, jnp.float32)
    if last:
        out_specs = row_spec
        out_shape = jax.ShapeDtypeStruct(queries.shape, jnp.bfloat16)
    else:
        out_specs = [row_spec] * 3
        out_shape = [row_f32] * 3
    carried = list(carry) if has_in else []
    grid_spec = pltpu.PrefetchScalarGridSpec(
        num_scalar_prefetch=2,
        grid=(heads, frames),
        in_specs=[row_spec, kv_spec] + [row_spec] * len(carried),
        out_specs=out_specs,
        scratch_shapes=[
            pltpu.VMEM((n_tiles, tile_size, tile_size), jnp.float32),
            pltpu.VMEM((tile_size, tile_size), jnp.float32),
            pltpu.VMEM((tile_size, tile_size), jnp.float32),
            pltpu.VMEM((tile_size, HD), jnp.float32),
        ],
    )
    tokens = queries.shape[0]
    cost = pl.CostEstimate(
        flops=4 * tokens * n_tiles * tile_size * local_width // 2,
        transcendentals=tokens * n_tiles * tile_size * heads // 2,
        bytes_accessed=(2 * n_tiles * tile_size + 4 * tokens) * local_width * 2,
    )
    return pl.pallas_call(
        kernel,
        grid_spec=grid_spec,
        out_shape=out_shape,
        cost_estimate=cost,
    )(order, count, queries, kv_all, *carried)


def shards(
    latent,
    query_weight,
    key_weight,
    value_weight,
    output_weight,
    query_gain,
    key_gain,
    modulation,
    noise_level,
    tile_pattern,
):
    frames, strip_rows, columns, local_width = latent.shape
    width = local_width * lax.axis_size("heads")
    token_count = frames * strip_rows * columns
    tile_size = strip_rows * columns
    levels = modulation.shape[0]
    rows = latent.reshape(token_count, local_width)
    whole = gather_heads(rows)
    onehot = (noise_level[0] == jnp.arange(levels, dtype=jnp.int32)).astype(jnp.float32)
    mod_table = jnp.dot(
        onehot[None, :], modulation.reshape(levels, 3 * width), precision=lax.Precision.HIGHEST
    ).reshape(3, width)
    token_rows = whole.astype(jnp.float32)
    center = token_rows - jnp.mean(token_rows, axis=1, keepdims=True)
    normed = center * lax.rsqrt(jnp.mean(center * center, axis=1, keepdims=True) + EPSILON)
    hidden = (normed * (1.0 + mod_table[1]) + mod_table[0]).astype(jnp.bfloat16)
    query_raw = jnp.dot(hidden, query_weight, preferred_element_type=jnp.float32)
    key_raw = jnp.dot(hidden, key_weight, preferred_element_type=jnp.float32)
    value_rows = jnp.dot(hidden, value_weight, preferred_element_type=jnp.float32).astype(
        jnp.bfloat16
    )
    key_squares = sum_pair(jnp.sum(key_raw * key_raw, axis=1))
    query_squares = sum_pair(jnp.sum(query_raw * query_raw, axis=1))
    queries = (query_raw * lax.rsqrt(query_squares / width + EPSILON)[:, None] * query_gain).astype(
        jnp.bfloat16
    )
    key_rows = (key_raw * lax.rsqrt(key_squares / width + EPSILON)[:, None] * key_gain).astype(
        jnp.bfloat16
    )
    kv = jnp.stack(
        [
            key_rows.reshape(frames, tile_size, local_width),
            value_rows.reshape(frames, tile_size, local_width),
        ]
    )
    own_low = from_behind(kv, "space", 1)
    own_high = from_behind(kv, "space", -1)
    prior_mid = from_behind(kv, "tm", 1)
    split = frames - frames // 3
    low_far = from_behind(prior_mid[:, :split], "space", 1)
    high_far = from_behind(prior_mid[:, :split], "space", -1)
    low_near = from_behind(own_low[:, split:], "tm", 1)
    high_near = from_behind(own_high[:, split:], "tm", 1)
    fr = list(range(frames))
    kv_list = [
        (low_far, [0 * frames + f for f in fr[:split]]),
        (low_near, [0 * frames + f for f in fr[split:]]),
        (prior_mid, [1 * frames + f for f in fr]),
        (high_far, [2 * frames + f for f in fr[:split]]),
        (high_near, [2 * frames + f for f in fr[split:]]),
        (own_low, [3 * frames + f for f in fr]),
        (kv, [4 * frames + f for f in fr]),
        (own_high, [5 * frames + f for f in fr]),
    ]
    pattern = jnp.transpose(tile_pattern[0].reshape(frames, 2, frames, 3), (0, 1, 3, 2))
    span_index = lax.axis_index("tm")
    strip_index = lax.axis_index("space")
    source_valid = jnp.stack([span_index > 0, jnp.array(True)])
    offset_valid = jnp.stack(
        [strip_index > 0, jnp.array(True), strip_index < lax.axis_size("space") - 1]
    )
    visible = (pattern > 0) & source_valid[None, :, None, None] & offset_valid[None, None, :, None]
    visible = visible.reshape(frames, 6 * frames).astype(jnp.int32)
    near = [kv_list[i] for i in (2, 5, 6, 7)]
    far = [kv_list[i] for i in (0, 1, 3, 4)]
    carry = attention(visible, queries, near, frames, tile_size, last=False)
    attended = attention(visible, queries, far, frames, tile_size, carry)
    column_start = lax.axis_index("heads") * local_width
    projected = output_columns(attended, output_weight, local_width)
    gate_half = lax.dynamic_slice_in_dim(mod_table[2], column_start, local_width)
    own_rows = rows.astype(jnp.float32)
    updated = (own_rows + gate_half * projected).astype(jnp.bfloat16)
    return updated.reshape(latent.shape)


def solution(mesh):
    placed = (
        P(("groups", "tm"), "space", None, "heads"),
        P(None, "heads"),
        P(None, "heads"),
        P(None, "heads"),
        P("heads", None),
        P("heads"),
        P("heads"),
        P(),
        P(("groups", "tm")),
        P("space", None, None, None),
    )
    return jax.shard_map(
        shards,
        mesh=mesh,
        in_specs=placed,
        out_specs=P(("groups", "tm"), "space", None, "heads"),
        check_vma=False,
    )
```

profile of v0, /device:TPU:11, one launch (start us, length us, event | category | flops | bytes accessed | tf_op | source)
XLA Modules:
  0.0 155.3 jit_solution(8553381954409377983)
XLA Ops:
  0.0 1.4 copy.19
  6.4 1.3 broadcast_select_fusion.1
  10.4 1.8 %multiply_reduce_fusion = (f32[624]{0:T(1024)S(1)}, f32[624,768]{1,0:T(8,128)S(1)}) fusion(bf16[624,1536]{1,0:T(8,128)(2,1)S(1)} %fusion.5, bf16[1536,768]{1,0:T(8,128)(2,1)S(1)} %copy-done.13), kind=kOutput, calls=%fused_computation.16 | convolution fusion | flops 1473158528 | bytes 6195648 | tf_op jit(solution)/shard_map/dot_general | solution.py:204
  12.8 1.6 %convolution_convert_fusion = bf16[624,768]{1,0:T(8,128)(2,1)S(1)} fusion(bf16[624,1536]{1,0:T(8,128)(2,1)S(1)} %fusion.5, bf16[1536,768]{1,0:T(8,128)(2,1)S(1)} %copy-done.14), kind=kOutput, calls=%fused_computation.19 | convolution fusion | flops 1472679936 | bytes 5234688 | tf_op jit(solution)/shard_map/dot_general | solution.py:205
  14.7 1.4 pad_maximum_fusion.3
  17.5 2.1 %collective-permute-start.8 = (bf16[2,3,208,768]{3,2,1,0:T(8,128)(2,1)}, bf16[2,3,208,768]{3,2,1,0:T(8,128)(2,1)}, u32[]{:S(2)}, u32[]{:S(2)}) collective-permute-start(bf16[2,3,208,768]{3,2,1,0:T(8,128)(2,1)} %pad_maximum_fusion.3), channel_id=1, source_target_pairs={{4,0},{8,4},{12,8},{5,1},{9,5},{13,9},{6,2},{10,6},{14,10},{7,3},{... | collective-permute-start | bytes 5750792 | tf_op jit(solution)/shard_map/ppermute | solution.py:20
  19.6 3.2 %collective-permute-start.5 = (bf16[2,3,208,768]{3,2,1,0:T(8,128)(2,1)}, bf16[2,3,208,768]{3,2,1,0:T(8,128)(2,1)}, u32[]{:S(2)}, u32[]{:S(2)}) collective-permute-start(bf16[2,3,208,768]{3,2,1,0:T(8,128)(2,1)} %pad_maximum_fusion.3), channel_id=1, source_target_pairs={{0,4},{4,8},{8,12},{1,5},{5,9},{9,13},{2,6},{6,10},{10,14},{3,7},{... | collective-permute-start | bytes 5750792 | tf_op jit(solution)/shard_map/ppermute | solution.py:20
  25.0 5.2 %multiply_reduce_fusion.1 = (f32[624]{0:T(1024)S(1)}, f32[624,768]{1,0:T(8,128)}) fusion(bf16[624,1536]{1,0:T(8,128)(2,1)} %copy-done.6, bf16[1536,768]{1,0:T(8,128)(2,1)} %param.13), kind=kOutput, calls=%fused_computation.18 | convolution fusion | flops 1473158528 | bytes 6195648 | tf_op jit(solution)/shard_map/dot_general | solution.py:203
  34.5 26.7 %collective-permute-done.3 = bf16[2,3,208,768]{3,2,1,0:T(8,128)(2,1)} collective-permute-done((bf16[2,3,208,768]{3,2,1,0:T(8,128)(2,1)}, bf16[2,3,208,768]{3,2,1,0:T(8,128)(2,1)}, u32[]{:S(2)}, u32[]{:S(2)}) %collective-permute-start.3) | collective-permute-done | bytes 1916960 | tf_op jit(solution)/shard_map/ppermute | solution.py:20
  61.2 2.4 %slice.35 = bf16[2,2,208,768]{3,2,1,0:T(8,128)(2,1)} slice(bf16[2,3,208,768]{3,2,1,0:T(8,128)(2,1)} %collective-permute-done.3), slice={[0:2], [0:2], [0:208], [0:768]} | slice | bytes 2555904 | tf_op jit(solution)/shard_map/slice | solution.py:226
  63.6 2.1 %collective-permute-start.7 = (bf16[2,2,208,768]{3,2,1,0:T(8,128)(2,1)}, bf16[2,2,208,768]{3,2,1,0:T(8,128)(2,1)}, u32[]{:S(2)}, u32[]{:S(2)}) collective-permute-start(bf16[2,2,208,768]{3,2,1,0:T(8,128)(2,1)} %slice.35), channel_id=1, source_target_pairs={{4,0},{8,4},{12,8},{5,1},{9,5},{13,9},{6,2},{10,6},{14,10},{7,3},{... | collective-permute-start | bytes 3833864 | tf_op jit(solution)/shard_map/ppermute | solution.py:20
  65.7 3.2 %collective-permute-start.4 = (bf16[2,2,208,768]{3,2,1,0:T(8,128)(2,1)}, bf16[2,2,208,768]{3,2,1,0:T(8,128)(2,1)}, u32[]{:S(2)}, u32[]{:S(2)}) collective-permute-start(bf16[2,2,208,768]{3,2,1,0:T(8,128)(2,1)} %slice.35), channel_id=1, source_target_pairs={{0,4},{4,8},{8,12},{1,5},{5,9},{9,13},{2,6},{6,10},{10,14},{3,7},{... | collective-permute-start | bytes 3833864 | tf_op jit(solution)/shard_map/ppermute | solution.py:20
  70.1 2.0 %slice.37 = bf16[2,1,208,768]{3,2,1,0:T(8,128)(2,1)} slice(bf16[2,3,208,768]{3,2,1,0:T(8,128)(2,1)} %collective-permute-done.8), slice={[0:2], [2:3], [0:208], [0:768]} | slice | bytes 1277952 | tf_op jit(solution)/shard_map/slice | solution.py:229
  73.5 2.0 %slice.36 = bf16[2,1,208,768]{3,2,1,0:T(8,128)(2,1)} slice(bf16[2,3,208,768]{3,2,1,0:T(8,128)(2,1)} %collective-permute-done.5), slice={[0:2], [2:3], [0:208], [0:768]} | slice | bytes 1277952 | tf_op jit(solution)/shard_map/slice | solution.py:228
  75.4 1.5 collective-permute-start.6
  76.9 6.5 %pad_maximum_fusion.refs_0_ = bf16[2,12,208,768]{3,2,1,0:T(8,128)(2,1)} fusion(bf16[2,3,208,768]{3,2,1,0:T(8,128)(2,1)} %collective-permute-done.8, bf16[1,3,208,768]{3,2,1,0:T(8,128)(2,1)S(1)} %bitcast.34, bf16[1,3,208,768]{3,2,1,0:T(8,128)(2,1)S(1)} %bitcast.32, bf16[2,3,208,768]{3,2,1,0:T(8,128)(2,1)} %collective-permute-done.5, ...), kind=kLoop, calls=%fused_computation.2 | loop fusion | flops 15335424 | bytes 15335424 | tf_op jit(solution)/shard_map/concatenate | solution.py:131
  83.4 30.0 %shard_map.118 = (f32[624,768]{1,0:T(8,128)}, f32[624,768]{1,0:T(8,128)}, f32[624,768]{1,0:T(8,128)}) custom-call(s32[3,12]{1,0:T(4,128)} %copy.25.order_ref, s32[3]{0:T(128)} %get-tuple-element.20.count_ref, bf16[624,768]{1,0:T(8,128)(2,1)} %multiply_convert_fusion.1.q_ref, bf16[2,12,208,768]{3,2,1,0:T(8,128)(2,1)} %pad_maximum_fusion.refs_0_), custom_call_target="tpu_custom_call" | custom-call | flops 2392326144 | bytes 11501568 | tf_op jit(solution)/shard_map/pallas_call | solution.py:168
  113.5 3.6 %pad_maximum_fusion.1.refs_0_ = bf16[2,6,208,768]{3,2,1,0:T(8,128)(2,1)} fusion(bf16[2,1,208,768]{3,2,1,0:T(8,128)(2,1)} %collective-permute-done.9, bf16[2,2,208,768]{3,2,1,0:T(8,128)(2,1)} %collective-permute-done.7, bf16[2,1,208,768]{3,2,1,0:T(8,128)(2,1)} %collective-permute-done.6, bf16[2,2,208,768]{3,2,1,0:T(8,128)(2,1)} %collective-permute-done.4), kind=kLoop, calls=%fused_computation.11 | loop fusion | flops 5750784 | bytes 7667712 | tf_op jit(solution)/shard_map/concatenate | solution.py:131
  117.0 27.3 %shard_map.119 = bf16[624,768]{1,0:T(8,128)(2,1)} custom-call(s32[3,6]{1,0:T(4,128)} %copy.26.order_ref, s32[3]{0:T(128)} %get-tuple-element.22.count_ref, bf16[624,768]{1,0:T(8,128)(2,1)} %multiply_convert_fusion.1.q_ref, bf16[2,6,208,768]{3,2,1,0:T(8,128)(2,1)} %pad_maximum_fusion.1.refs_0_, f32[624,768]{1,0:T(8,128)} %get-tuple-element.12.refs_1_, ...), custom_call_target="tpu_custom_call" | custom-call | flops 1196163072 | bytes 7667712 | tf_op jit(solution)/shard_map/pallas_call | solution.py:168
  144.3 1.9 %collective-permute-start.10 = (bf16[624,768]{1,0:T(8,128)(2,1)}, bf16[624,768]{1,0:T(8,128)(2,1)S(1)}, u32[]{:S(2)}, u32[]{:S(2)}) collective-permute-start(bf16[624,768]{1,0:T(8,128)(2,1)} %shard_map.119), channel_id=1, source_target_pairs={{0,1},{1,0},{2,3},{3,2},{4,5},{5,4},{6,7},{7,6},{8,9},{9,8},{10,11... | collective-permute-start | bytes 2875400 | tf_op jit(solution)/shard_map/ppermute | solution.py:57
  146.3 2.3 %collective-permute-done.10 = bf16[624,768]{1,0:T(8,128)(2,1)S(1)} collective-permute-done((bf16[624,768]{1,0:T(8,128)(2,1)}, bf16[624,768]{1,0:T(8,128)(2,1)S(1)}, u32[]{:S(2)}, u32[]{:S(2)}) %collective-permute-start.10) | collective-permute-done | bytes 958496 | tf_op jit(solution)/shard_map/ppermute | solution.py:57
  148.6 2.2 %fusion.15 = f32[624,768]{1,0:T(8,128)S(1)} fusion(bf16[624,768]{1,0:T(8,128)(2,1)S(1)} %collective-permute-done.10, bf16[768,768]{1,0:T(8,128)(2,1)} %collective-permute-done.11), kind=kOutput, calls=%fused_computation.46 | convolution fusion | flops 736100352 | bytes 4055040 | tf_op jit(solution)/shard_map/dot_general | solution.py:58
  150.8 1.9 %add_convert_fusion = bf16[624,768]{1,0:T(8,128)(2,1)} fusion(f32[624,768]{1,0:T(8,128)S(1)} %fusion.15, bf16[624,768]{1,0:T(8,128)(2,1)S(1)} %copy-done.2, bf16[624,768]{1,0:T(8,128)(2,1)S(1)} %copy-done.7, bf16[768,1536]{1,0:T(8,128)(2,1)S(1)} %copy-done, s32[]{:T(128)S(6)} %select_n.25, f32[768]{0:T(1024)S(1)} %dynamic_slice.9), kind=kOutput, calls=%fused_computation.14 | convolution fusion | flops 738496512 | bytes 5976068 | tf_op jit(solution)/shard_map/dot_general | solution.py:58
  154.0 1.3 copy.27
  (81 shorter events, 19.4 us)
Async XLA Ops:
  0.0 3.2 %copy-start = (bf16[768,1536]{1,0:T(8,128)(2,1)S(1)}, bf16[768,1536]{1,0:T(8,128)(2,1)}, u32[]{:S(2)}) copy-start(bf16[768,1536]{1,0:T(8,128)(2,1)} %param.16) | copy-start | bytes 7077892
  2.6 3.8 %copy-start.1 = (bf16[624,768]{1,0:T(8,128)(2,1)S(1)}, bf16[624,768]{1,0:T(8,128)(2,1)}, u32[]{:S(2)}) copy-start(bf16[624,768]{1,0:T(8,128)(2,1)} %reshape.51) | copy-start | bytes 2875396
  2.6 3.8 %collective-permute-start = (bf16[624,768]{1,0:T(8,128)(2,1)}, bf16[624,768]{1,0:T(8,128)(2,1)}, u32[]{:S(2)}, u32[]{:S(2)}) collective-permute-start(bf16[624,768]{1,0:T(8,128)(2,1)} %reshape.51), channel_id=1, source_target_pairs={{0,1},{1,0},{2,3},{3,2},{4,5},{5,4},{6,7},{7,6},{8,9},{9,8},{10,11... | collective-permute-start | bytes 2875400 | tf_op jit(solution)/shard_map/ppermute | solution.py:27
  4.4 141.9 %collective-permute-start.11 = (bf16[768,768]{1,0:T(8,128)(2,1)}, bf16[768,768]{1,0:T(8,128)(2,1)}, u32[]{:S(2)}, u32[]{:S(2)}) collective-permute-start(bf16[768,768]{1,0:T(8,128)(2,1)} %constant_dynamic-slice_fusion), channel_id=1, source_target_pairs={{0,1},{1,0},{2,3},{3,2},{4,5},{5,4},{6,7},{7,6},{8,9},{9,8},{10,11... | collective-permute-start | bytes 3538952 | tf_op jit(solution)/shard_map/ppermute | solution.py:56
  10.4 2.3 %copy-start.6 = (bf16[624,1536]{1,0:T(8,128)(2,1)}, bf16[624,1536]{1,0:T(8,128)(2,1)S(1)}, u32[]{:S(2)}) copy-start(bf16[624,1536]{1,0:T(8,128)(2,1)S(1)} %fusion.5) | copy-start | bytes 5750788
  10.4 2.4 %copy-start.14 = (bf16[1536,768]{1,0:T(8,128)(2,1)S(1)}, bf16[1536,768]{1,0:T(8,128)(2,1)}, u32[]{:S(2)}) copy-start(bf16[1536,768]{1,0:T(8,128)(2,1)} %param.15) | copy-start | bytes 7077892
  12.2 2.3 %collective-permute-start.2 = (f32[624]{0:T(1024)S(1)}, f32[624]{0:T(1024)S(1)}, u32[]{:S(2)}, u32[]{:S(2)}) collective-permute-start(f32[624]{0:T(1024)S(1)} %get-tuple-element.26), channel_id=1, source_target_pairs={{0,1},{1,0},{2,3},{3,2},{4,5},{5,4},{6,7},{7,6},{8,9},{9,8},{10,11... | collective-permute-start | bytes 7496 | tf_op jit(solution)/shard_map/ppermute | solution.py:45
  14.7 2.8 %copy-start.8 = (s32[1,3,6,3]{2,0,3,1:T(1,128)S(1)}, s32[1,3,6,3]{2,0,3,1:T(1,128)}, u32[]{:S(2)}) copy-start(s32[1,3,6,3]{2,0,3,1:T(1,128)} %param.21) | copy-start | bytes 652
  14.7 8.5 %copy-start.12 = (s32[6]{0:T(128)S(1)}, s32[6]{0:T(128)}, u32[]{:S(2)}) copy-start(s32[6]{0:T(128)} %constant.63) | copy-start | bytes 76
  14.7 9.1 %copy-start.11 = (s32[12]{0:T(128)S(1)}, s32[12]{0:T(128)}, u32[]{:S(2)}) copy-start(s32[12]{0:T(128)} %constant.64) | copy-start | bytes 148
  16.2 45.0 %collective-permute-start.3 = (bf16[2,3,208,768]{3,2,1,0:T(8,128)(2,1)}, bf16[2,3,208,768]{3,2,1,0:T(8,128)(2,1)}, u32[]{:S(2)}, u32[]{:S(2)}) collective-permute-start(bf16[2,3,208,768]{3,2,1,0:T(8,128)(2,1)} %pad_maximum_fusion.3), channel_id=1, source_target_pairs={{0,2},{1,3},{4,6},{5,7},{8,10},{9,11},{12,14},{13,15},{16,18},{17,... | collective-permute-start | bytes 5750792 | tf_op jit(solution)/shard_map/ppermute | solution.py:20
  17.5 52.6 %collective-permute-start.8 = (bf16[2,3,208,768]{3,2,1,0:T(8,128)(2,1)}, bf16[2,3,208,768]{3,2,1,0:T(8,128)(2,1)}, u32[]{:S(2)}, u32[]{:S(2)}) collective-permute-start(bf16[2,3,208,768]{3,2,1,0:T(8,128)(2,1)} %pad_maximum_fusion.3), channel_id=1, source_target_pairs={{4,0},{8,4},{12,8},{5,1},{9,5},{13,9},{6,2},{10,6},{14,10},{7,3},{... | collective-permute-start | bytes 5750792 | tf_op jit(solution)/shard_map/ppermute | solution.py:20
  19.6 53.9 %collective-permute-start.5 = (bf16[2,3,208,768]{3,2,1,0:T(8,128)(2,1)}, bf16[2,3,208,768]{3,2,1,0:T(8,128)(2,1)}, u32[]{:S(2)}, u32[]{:S(2)}) collective-permute-start(bf16[2,3,208,768]{3,2,1,0:T(8,128)(2,1)} %pad_maximum_fusion.3), channel_id=1, source_target_pairs={{0,4},{4,8},{8,12},{1,5},{5,9},{9,13},{2,6},{6,10},{10,14},{3,7},{... | collective-permute-start | bytes 5750792 | tf_op jit(solution)/shard_map/ppermute | solution.py:20
  30.1 38.8 %copy-start.10 = (f32[768]{0:T(1024)S(1)}, f32[768]{0:T(1024)}, u32[]{:S(2)}) copy-start(f32[768]{0:T(1024)} %param.17) | copy-start | bytes 9220
  30.1 4.3 %collective-permute-start.1 = (f32[624]{0:T(1024)S(1)}, f32[624]{0:T(1024)S(1)}, u32[]{:S(2)}, u32[]{:S(2)}) collective-permute-start(f32[624]{0:T(1024)S(1)} %get-tuple-element.24), channel_id=1, source_target_pairs={{0,1},{1,0},{2,3},{3,2},{4,5},{5,4},{6,7},{7,6},{8,9},{9,8},{10,11... | collective-permute-start | bytes 7496 | tf_op jit(solution)/shard_map/ppermute | solution.py:45
  34.5 34.5 %copy-start.5 = (f32[624,768]{1,0:T(8,128)S(1)}, f32[624,768]{1,0:T(8,128)}, u32[]{:S(2)}) copy-start(f32[624,768]{1,0:T(8,128)} %get-tuple-element.25) | copy-start | bytes 5750788
  63.6 49.8 %collective-permute-start.7 = (bf16[2,2,208,768]{3,2,1,0:T(8,128)(2,1)}, bf16[2,2,208,768]{3,2,1,0:T(8,128)(2,1)}, u32[]{:S(2)}, u32[]{:S(2)}) collective-permute-start(bf16[2,2,208,768]{3,2,1,0:T(8,128)(2,1)} %slice.35), channel_id=1, source_target_pairs={{4,0},{8,4},{12,8},{5,1},{9,5},{13,9},{6,2},{10,6},{14,10},{7,3},{... | collective-permute-start | bytes 3833864 | tf_op jit(solution)/shard_map/ppermute | solution.py:20
  65.7 47.7 %collective-permute-start.4 = (bf16[2,2,208,768]{3,2,1,0:T(8,128)(2,1)}, bf16[2,2,208,768]{3,2,1,0:T(8,128)(2,1)}, u32[]{:S(2)}, u32[]{:S(2)}) collective-permute-start(bf16[2,2,208,768]{3,2,1,0:T(8,128)(2,1)} %slice.35), channel_id=1, source_target_pairs={{0,4},{4,8},{8,12},{1,5},{5,9},{9,13},{2,6},{6,10},{10,14},{3,7},{... | collective-permute-start | bytes 3833864 | tf_op jit(solution)/shard_map/ppermute | solution.py:20
  70.1 6.8 %copy-start.4 = (bf16[624,768]{1,0:T(8,128)(2,1)S(1)}, bf16[624,768]{1,0:T(8,128)(2,1)}, u32[]{:S(2)}) copy-start(bf16[624,768]{1,0:T(8,128)(2,1)} %copy-done.3) | copy-start | bytes 2875396
  72.2 41.3 %collective-permute-start.9 = (bf16[2,1,208,768]{3,2,1,0:T(8,128)(2,1)}, bf16[2,1,208,768]{3,2,1,0:T(8,128)(2,1)}, u32[]{:S(2)}, u32[]{:S(2)}) collective-permute-start(bf16[2,1,208,768]{3,2,1,0:T(8,128)(2,1)} %slice.37), channel_id=1, source_target_pairs={{0,2},{1,3},{4,6},{5,7},{8,10},{9,11},{12,14},{13,15},{16,18},{17,... | collective-permute-start | bytes 1916936 | tf_op jit(solution)/shard_map/ppermute | solution.py:20
  75.4 38.0 %collective-permute-start.6 = (bf16[2,1,208,768]{3,2,1,0:T(8,128)(2,1)}, bf16[2,1,208,768]{3,2,1,0:T(8,128)(2,1)}, u32[]{:S(2)}, u32[]{:S(2)}) collective-permute-start(bf16[2,1,208,768]{3,2,1,0:T(8,128)(2,1)} %slice.36), channel_id=1, source_target_pairs={{0,2},{1,3},{4,6},{5,7},{8,10},{9,11},{12,14},{13,15},{16,18},{17,... | collective-permute-start | bytes 1916936 | tf_op jit(solution)/shard_map/ppermute | solution.py:20
  144.3 4.3 %collective-permute-start.10 = (bf16[624,768]{1,0:T(8,128)(2,1)}, bf16[624,768]{1,0:T(8,128)(2,1)S(1)}, u32[]{:S(2)}, u32[]{:S(2)}) collective-permute-start(bf16[624,768]{1,0:T(8,128)(2,1)} %shard_map.119), channel_id=1, source_target_pairs={{0,1},{1,0},{2,3},{3,2},{4,5},{5,4},{6,7},{7,6},{8,9},{9,8},{10,11... | collective-permute-start | bytes 2875400 | tf_op jit(solution)/shard_map/ppermute | solution.py:57
  146.3 4.5 %copy-start.2 = (bf16[624,768]{1,0:T(8,128)(2,1)S(1)}, bf16[624,768]{1,0:T(8,128)(2,1)}, u32[]{:S(2)}) copy-start(bf16[624,768]{1,0:T(8,128)(2,1)} %reshape.51) | copy-start | bytes 2875396
  146.3 4.5 %copy-start.7 = (bf16[624,768]{1,0:T(8,128)(2,1)S(1)}, bf16[624,768]{1,0:T(8,128)(2,1)}, u32[]{:S(2)}) copy-start(bf16[624,768]{1,0:T(8,128)(2,1)} %shard_map.119) | copy-start | bytes 2875396
  (3 other events, 5.7 us)
where the time goes:
time: 156 us; the launch traced here: 155 us
  Pallas kernels  57.3 us (37%)
  waiting for transfers between devices  29 us (19%)
  starting transfers between devices  18.8 us (12%)
  other arithmetic  18.8 us (12%)
  local copies, waits for them, and re-layouts  17.5 us (11%)
  matrix products  12.9 us (8%)
    pallas_call x2, Pallas kernels, attention(): pl.pallas_call(kernel, grid_spec=grid_spec, out_shape=out_shape, cost_est...  57.3 us
    ppermute x7, waiting for transfers between devices, from_behind(): lax.ppermute(value, axis, [(source, source + steps) for source in range(f...  26.7 us
    ppermute x7, starting transfers between devices, from_behind(): lax.ppermute(value, axis, [(source, source + steps) for source in range(f...  14.6 us
    concatenate x2, other arithmetic, attention(): kv_all = jnp.concatenate([kv for kv, _ in kv_list], axis=1)  10.1 us
    dot_general x1, matrix products, shards(): jnp.dot(hidden, query_weight, preferred_element_type=jnp.float32)  5.17 us
  transfers between devices with their start and end apart: 12, of which 2 were waited for; matrix products, arithmetic and copies ran while one was open for 25% of the time, Pallas kernels for 37%

commit v1 on v0

--- a/solution.py
+++ b/solution.py
@@ -133,7 +133,7 @@
     order = jnp.argsort(1 - seen, axis=1, stable=True).astype(jnp.int32)
     count = jnp.sum(seen, axis=1).astype(jnp.int32)
     has_in = carry is not None
-    group_size = n_tiles if n_tiles >= 4 * GROUP else GROUP
+    group_size = n_tiles
     kernel = functools.partial(
         attention_kernel, 1.0 / math.sqrt(HD), n_tiles, group_size, has_in, not last
     )

time: 156 us -> 157 us (level)
  no operation moved by 1% of the time
where the time goes in v1:
time: 157 us; the launch traced here: 155 us
  Pallas kernels  56.8 us (36%)
  waiting for transfers between devices  29 us (18%)
  starting transfers between devices  18.8 us (12%)
  other arithmetic  18.8 us (12%)
  local copies, waits for them, and re-layouts  17.5 us (11%)
  matrix products  12.9 us (8%)
    pallas_call x2, Pallas kernels, attention(): pl.pallas_call(kernel, grid_spec=grid_spec, out_shape=out_shape, cost_est...  56.8 us
    ppermute x7, waiting for transfers between devices, from_behind(): lax.ppermute(value, axis, [(source, source + steps) for source in range(f...  26.7 us
    ppermute x7, starting transfers between devices, from_behind(): lax.ppermute(value, axis, [(source, source + steps) for source in range(f...  14.6 us
    concatenate x2, other arithmetic, attention(): kv_all = jnp.concatenate([kv for kv, _ in kv_list], axis=1)  10.1 us
    dot_general x1, matrix products, shards(): jnp.dot(hidden, query_weight, preferred_element_type=jnp.float32)  5.17 us
  transfers between devices with their start and end apart: 12, of which 2 were waited for; matrix products, arithmetic and copies ran while one was open for 25% of the time, Pallas kernels for 37%

profile of v1, /device:TPU:11, one launch (start us, length us, event | category | flops | bytes accessed | tf_op | source)
XLA Modules:
  0.0 154.8 jit_solution(4749484217832747519)
XLA Ops:
  0.0 1.4 copy.19
  6.4 1.3 broadcast_select_fusion.1
  10.4 1.8 %multiply_reduce_fusion = (f32[624]{0:T(1024)S(1)}, f32[624,768]{1,0:T(8,128)S(1)}) fusion(bf16[624,1536]{1,0:T(8,128)(2,1)S(1)} %fusion.5, bf16[1536,768]{1,0:T(8,128)(2,1)S(1)} %copy-done.13), kind=kOutput, calls=%fused_computation.16 | convolution fusion | flops 1473158528 | bytes 6195648 | tf_op jit(solution)/shard_map/dot_general | solution.py:204
  12.8 1.6 %convolution_convert_fusion = bf16[624,768]{1,0:T(8,128)(2,1)S(1)} fusion(bf16[624,1536]{1,0:T(8,128)(2,1)S(1)} %fusion.5, bf16[1536,768]{1,0:T(8,128)(2,1)S(1)} %copy-done.14), kind=kOutput, calls=%fused_computation.19 | convolution fusion | flops 1472679936 | bytes 5234688 | tf_op jit(solution)/shard_map/dot_general | solution.py:205
  14.7 1.4 pad_maximum_fusion.3
  17.5 2.1 %collective-permute-start.8 = (bf16[2,3,208,768]{3,2,1,0:T(8,128)(2,1)}, bf16[2,3,208,768]{3,2,1,0:T(8,128)(2,1)}, u32[]{:S(2)}, u32[]{:S(2)}) collective-permute-start(bf16[2,3,208,768]{3,2,1,0:T(8,128)(2,1)} %pad_maximum_fusion.3), channel_id=1, source_target_pairs={{4,0},{8,4},{12,8},{5,1},{9,5},{13,9},{6,2},{10,6},{14,10},{7,3},{... | collective-permute-start | bytes 5750792 | tf_op jit(solution)/shard_map/ppermute | solution.py:20
  19.6 3.2 %collective-permute-start.5 = (bf16[2,3,208,768]{3,2,1,0:T(8,128)(2,1)}, bf16[2,3,208,768]{3,2,1,0:T(8,128)(2,1)}, u32[]{:S(2)}, u32[]{:S(2)}) collective-permute-start(bf16[2,3,208,768]{3,2,1,0:T(8,128)(2,1)} %pad_maximum_fusion.3), channel_id=1, source_target_pairs={{0,4},{4,8},{8,12},{1,5},{5,9},{9,13},{2,6},{6,10},{10,14},{3,7},{... | collective-permute-start | bytes 5750792 | tf_op jit(solution)/shard_map/ppermute | solution.py:20
  25.0 5.2 %multiply_reduce_fusion.1 = (f32[624]{0:T(1024)S(1)}, f32[624,768]{1,0:T(8,128)}) fusion(bf16[624,1536]{1,0:T(8,128)(2,1)} %copy-done.6, bf16[1536,768]{1,0:T(8,128)(2,1)} %param.13), kind=kOutput, calls=%fused_computation.18 | convolution fusion | flops 1473158528 | bytes 6195648 | tf_op jit(solution)/shard_map/dot_general | solution.py:203
  34.5 26.7 %collective-permute-done.3 = bf16[2,3,208,768]{3,2,1,0:T(8,128)(2,1)} collective-permute-done((bf16[2,3,208,768]{3,2,1,0:T(8,128)(2,1)}, bf16[2,3,208,768]{3,2,1,0:T(8,128)(2,1)}, u32[]{:S(2)}, u32[]{:S(2)}) %collective-permute-start.3) | collective-permute-done | bytes 1916960 | tf_op jit(solution)/shard_map/ppermute | solution.py:20
  61.2 2.4 %slice.35 = bf16[2,2,208,768]{3,2,1,0:T(8,128)(2,1)} slice(bf16[2,3,208,768]{3,2,1,0:T(8,128)(2,1)} %collective-permute-done.3), slice={[0:2], [0:2], [0:208], [0:768]} | slice | bytes 2555904 | tf_op jit(solution)/shard_map/slice | solution.py:226
  63.6 2.1 %collective-permute-start.7 = (bf16[2,2,208,768]{3,2,1,0:T(8,128)(2,1)}, bf16[2,2,208,768]{3,2,1,0:T(8,128)(2,1)}, u32[]{:S(2)}, u32[]{:S(2)}) collective-permute-start(bf16[2,2,208,768]{3,2,1,0:T(8,128)(2,1)} %slice.35), channel_id=1, source_target_pairs={{4,0},{8,4},{12,8},{5,1},{9,5},{13,9},{6,2},{10,6},{14,10},{7,3},{... | collective-permute-start | bytes 3833864 | tf_op jit(solution)/shard_map/ppermute | solution.py:20
  65.7 3.2 %collective-permute-start.4 = (bf16[2,2,208,768]{3,2,1,0:T(8,128)(2,1)}, bf16[2,2,208,768]{3,2,1,0:T(8,128)(2,1)}, u32[]{:S(2)}, u32[]{:S(2)}) collective-permute-start(bf16[2,2,208,768]{3,2,1,0:T(8,128)(2,1)} %slice.35), channel_id=1, source_target_pairs={{0,4},{4,8},{8,12},{1,5},{5,9},{9,13},{2,6},{6,10},{10,14},{3,7},{... | collective-permute-start | bytes 3833864 | tf_op jit(solution)/shard_map/ppermute | solution.py:20
  70.1 2.0 %slice.37 = bf16[2,1,208,768]{3,2,1,0:T(8,128)(2,1)} slice(bf16[2,3,208,768]{3,2,1,0:T(8,128)(2,1)} %collective-permute-done.8), slice={[0:2], [2:3], [0:208], [0:768]} | slice | bytes 1277952 | tf_op jit(solution)/shard_map/slice | solution.py:229
  73.5 2.0 %slice.36 = bf16[2,1,208,768]{3,2,1,0:T(8,128)(2,1)} slice(bf16[2,3,208,768]{3,2,1,0:T(8,128)(2,1)} %collective-permute-done.5), slice={[0:2], [2:3], [0:208], [0:768]} | slice | bytes 1277952 | tf_op jit(solution)/shard_map/slice | solution.py:228
  75.4 1.5 collective-permute-start.6
  76.9 6.5 %pad_maximum_fusion.refs_0_ = bf16[2,12,208,768]{3,2,1,0:T(8,128)(2,1)} fusion(bf16[2,3,208,768]{3,2,1,0:T(8,128)(2,1)} %collective-permute-done.8, bf16[1,3,208,768]{3,2,1,0:T(8,128)(2,1)S(1)} %bitcast.34, bf16[1,3,208,768]{3,2,1,0:T(8,128)(2,1)S(1)} %bitcast.32, bf16[2,3,208,768]{3,2,1,0:T(8,128)(2,1)} %collective-permute-done.5, ...), kind=kLoop, calls=%fused_computation.2 | loop fusion | flops 15335424 | bytes 15335424 | tf_op jit(solution)/shard_map/concatenate | solution.py:131
  83.4 30.0 %shard_map.118 = (f32[624,768]{1,0:T(8,128)}, f32[624,768]{1,0:T(8,128)}, f32[624,768]{1,0:T(8,128)}) custom-call(s32[3,12]{1,0:T(4,128)} %copy.25.order_ref, s32[3]{0:T(128)} %get-tuple-element.20.count_ref, bf16[624,768]{1,0:T(8,128)(2,1)} %multiply_convert_fusion.1.q_ref, bf16[2,12,208,768]{3,2,1,0:T(8,128)(2,1)} %pad_maximum_fusion.refs_0_), custom_call_target="tpu_custom_call" | custom-call | flops 2392326144 | bytes 11501568 | tf_op jit(solution)/shard_map/pallas_call | solution.py:168
  113.4 3.6 %pad_maximum_fusion.1.refs_0_ = bf16[2,6,208,768]{3,2,1,0:T(8,128)(2,1)} fusion(bf16[2,1,208,768]{3,2,1,0:T(8,128)(2,1)} %collective-permute-done.9, bf16[2,2,208,768]{3,2,1,0:T(8,128)(2,1)} %collective-permute-done.7, bf16[2,1,208,768]{3,2,1,0:T(8,128)(2,1)} %collective-permute-done.6, bf16[2,2,208,768]{3,2,1,0:T(8,128)(2,1)} %collective-permute-done.4), kind=kLoop, calls=%fused_computation.11 | loop fusion | flops 5750784 | bytes 7667712 | tf_op jit(solution)/shard_map/concatenate | solution.py:131
  117.0 26.8 %shard_map.119 = bf16[624,768]{1,0:T(8,128)(2,1)} custom-call(s32[3,6]{1,0:T(4,128)} %copy.26.order_ref, s32[3]{0:T(128)} %get-tuple-element.22.count_ref, bf16[624,768]{1,0:T(8,128)(2,1)} %multiply_convert_fusion.1.q_ref, bf16[2,6,208,768]{3,2,1,0:T(8,128)(2,1)} %pad_maximum_fusion.1.refs_0_, f32[624,768]{1,0:T(8,128)} %get-tuple-element.12.refs_1_, ...), custom_call_target="tpu_custom_call" | custom-call | flops 1196163072 | bytes 7667712 | tf_op jit(solution)/shard_map/pallas_call | solution.py:168
  143.8 1.9 %collective-permute-start.10 = (bf16[624,768]{1,0:T(8,128)(2,1)}, bf16[624,768]{1,0:T(8,128)(2,1)S(1)}, u32[]{:S(2)}, u32[]{:S(2)}) collective-permute-start(bf16[624,768]{1,0:T(8,128)(2,1)} %shard_map.119), channel_id=1, source_target_pairs={{0,1},{1,0},{2,3},{3,2},{4,5},{5,4},{6,7},{7,6},{8,9},{9,8},{10,11... | collective-permute-start | bytes 2875400 | tf_op jit(solution)/shard_map/ppermute | solution.py:57
  145.8 2.3 %collective-permute-done.10 = bf16[624,768]{1,0:T(8,128)(2,1)S(1)} collective-permute-done((bf16[624,768]{1,0:T(8,128)(2,1)}, bf16[624,768]{1,0:T(8,128)(2,1)S(1)}, u32[]{:S(2)}, u32[]{:S(2)}) %collective-permute-start.10) | collective-permute-done | bytes 958496 | tf_op jit(solution)/shard_map/ppermute | solution.py:57
  148.1 2.2 %fusion.15 = f32[624,768]{1,0:T(8,128)S(1)} fusion(bf16[624,768]{1,0:T(8,128)(2,1)S(1)} %collective-permute-done.10, bf16[768,768]{1,0:T(8,128)(2,1)} %collective-permute-done.11), kind=kOutput, calls=%fused_computation.46 | convolution fusion | flops 736100352 | bytes 4055040 | tf_op jit(solution)/shard_map/dot_general | solution.py:58
  150.3 1.9 %add_convert_fusion = bf16[624,768]{1,0:T(8,128)(2,1)} fusion(f32[624,768]{1,0:T(8,128)S(1)} %fusion.15, bf16[624,768]{1,0:T(8,128)(2,1)S(1)} %copy-done.2, bf16[624,768]{1,0:T(8,128)(2,1)S(1)} %copy-done.7, bf16[768,1536]{1,0:T(8,128)(2,1)S(1)} %copy-done, s32[]{:T(128)S(6)} %select_n.25, f32[768]{0:T(1024)S(1)} %dynamic_slice.9), kind=kOutput, calls=%fused_computation.14 | convolution fusion | flops 738496512 | bytes 5976068 | tf_op jit(solution)/shard_map/dot_general | solution.py:58
  153.5 1.3 copy.27
  (81 shorter events, 19.4 us)
Async XLA Ops:
  0.0 3.2 %copy-start = (bf16[768,1536]{1,0:T(8,128)(2,1)S(1)}, bf16[768,1536]{1,0:T(8,128)(2,1)}, u32[]{:S(2)}) copy-start(bf16[768,1536]{1,0:T(8,128)(2,1)} %param.16) | copy-start | bytes 7077892
  2.6 3.8 %copy-start.1 = (bf16[624,768]{1,0:T(8,128)(2,1)S(1)}, bf16[624,768]{1,0:T(8,128)(2,1)}, u32[]{:S(2)}) copy-start(bf16[624,768]{1,0:T(8,128)(2,1)} %reshape.51) | copy-start | bytes 2875396
  2.6 3.8 %collective-permute-start = (bf16[624,768]{1,0:T(8,128)(2,1)}, bf16[624,768]{1,0:T(8,128)(2,1)}, u32[]{:S(2)}, u32[]{:S(2)}) collective-permute-start(bf16[624,768]{1,0:T(8,128)(2,1)} %reshape.51), channel_id=1, source_target_pairs={{0,1},{1,0},{2,3},{3,2},{4,5},{5,4},{6,7},{7,6},{8,9},{9,8},{10,11... | collective-permute-start | bytes 2875400 | tf_op jit(solution)/shard_map/ppermute | solution.py:27
  4.4 141.4 %collective-permute-start.11 = (bf16[768,768]{1,0:T(8,128)(2,1)}, bf16[768,768]{1,0:T(8,128)(2,1)}, u32[]{:S(2)}, u32[]{:S(2)}) collective-permute-start(bf16[768,768]{1,0:T(8,128)(2,1)} %constant_dynamic-slice_fusion), channel_id=1, source_target_pairs={{0,1},{1,0},{2,3},{3,2},{4,5},{5,4},{6,7},{7,6},{8,9},{9,8},{10,11... | collective-permute-start | bytes 3538952 | tf_op jit(solution)/shard_map/ppermute | solution.py:56
  10.4 2.3 %copy-start.6 = (bf16[624,1536]{1,0:T(8,128)(2,1)}, bf16[624,1536]{1,0:T(8,128)(2,1)S(1)}, u32[]{:S(2)}) copy-start(bf16[624,1536]{1,0:T(8,128)(2,1)S(1)} %fusion.5) | copy-start | bytes 5750788
  10.4 2.4 %copy-start.14 = (bf16[1536,768]{1,0:T(8,128)(2,1)S(1)}, bf16[1536,768]{1,0:T(8,128)(2,1)}, u32[]{:S(2)}) copy-start(bf16[1536,768]{1,0:T(8,128)(2,1)} %param.15) | copy-start | bytes 7077892
  12.2 2.3 %collective-permute-start.2 = (f32[624]{0:T(1024)S(1)}, f32[624]{0:T(1024)S(1)}, u32[]{:S(2)}, u32[]{:S(2)}) collective-permute-start(f32[624]{0:T(1024)S(1)} %get-tuple-element.26), channel_id=1, source_target_pairs={{0,1},{1,0},{2,3},{3,2},{4,5},{5,4},{6,7},{7,6},{8,9},{9,8},{10,11... | collective-permute-start | bytes 7496 | tf_op jit(solution)/shard_map/ppermute | solution.py:45
  14.7 2.8 %copy-start.8 = (s32[1,3,6,3]{2,0,3,1:T(1,128)S(1)}, s32[1,3,6,3]{2,0,3,1:T(1,128)}, u32[]{:S(2)}) copy-start(s32[1,3,6,3]{2,0,3,1:T(1,128)} %param.21) | copy-start | bytes 652
  14.7 8.5 %copy-start.12 = (s32[6]{0:T(128)S(1)}, s32[6]{0:T(128)}, u32[]{:S(2)}) copy-start(s32[6]{0:T(128)} %constant.63) | copy-start | bytes 76
  14.7 9.1 %copy-start.11 = (s32[12]{0:T(128)S(1)}, s32[12]{0:T(128)}, u32[]{:S(2)}) copy-start(s32[12]{0:T(128)} %constant.64) | copy-start | bytes 148
  16.2 45.0 %collective-permute-start.3 = (bf16[2,3,208,768]{3,2,1,0:T(8,128)(2,1)}, bf16[2,3,208,768]{3,2,1,0:T(8,128)(2,1)}, u32[]{:S(2)}, u32[]{:S(2)}) collective-permute-start(bf16[2,3,208,768]{3,2,1,0:T(8,128)(2,1)} %pad_maximum_fusion.3), channel_id=1, source_target_pairs={{0,2},{1,3},{4,6},{5,7},{8,10},{9,11},{12,14},{13,15},{16,18},{17,... | collective-permute-start | bytes 5750792 | tf_op jit(solution)/shard_map/ppermute | solution.py:20
  17.5 52.6 %collective-permute-start.8 = (bf16[2,3,208,768]{3,2,1,0:T(8,128)(2,1)}, bf16[2,3,208,768]{3,2,1,0:T(8,128)(2,1)}, u32[]{:S(2)}, u32[]{:S(2)}) collective-permute-start(bf16[2,3,208,768]{3,2,1,0:T(8,128)(2,1)} %pad_maximum_fusion.3), channel_id=1, source_target_pairs={{4,0},{8,4},{12,8},{5,1},{9,5},{13,9},{6,2},{10,6},{14,10},{7,3},{... | collective-permute-start | bytes 5750792 | tf_op jit(solution)/shard_map/ppermute | solution.py:20
  19.6 53.9 %collective-permute-start.5 = (bf16[2,3,208,768]{3,2,1,0:T(8,128)(2,1)}, bf16[2,3,208,768]{3,2,1,0:T(8,128)(2,1)}, u32[]{:S(2)}, u32[]{:S(2)}) collective-permute-start(bf16[2,3,208,768]{3,2,1,0:T(8,128)(2,1)} %pad_maximum_fusion.3), channel_id=1, source_target_pairs={{0,4},{4,8},{8,12},{1,5},{5,9},{9,13},{2,6},{6,10},{10,14},{3,7},{... | collective-permute-start | bytes 5750792 | tf_op jit(solution)/shard_map/ppermute | solution.py:20
  30.1 38.8 %copy-start.10 = (f32[768]{0:T(1024)S(1)}, f32[768]{0:T(1024)}, u32[]{:S(2)}) copy-start(f32[768]{0:T(1024)} %param.17) | copy-start | bytes 9220
  30.1 4.3 %collective-permute-start.1 = (f32[624]{0:T(1024)S(1)}, f32[624]{0:T(1024)S(1)}, u32[]{:S(2)}, u32[]{:S(2)}) collective-permute-start(f32[624]{0:T(1024)S(1)} %get-tuple-element.24), channel_id=1, source_target_pairs={{0,1},{1,0},{2,3},{3,2},{4,5},{5,4},{6,7},{7,6},{8,9},{9,8},{10,11... | collective-permute-start | bytes 7496 | tf_op jit(solution)/shard_map/ppermute | solution.py:45
  34.5 34.5 %copy-start.5 = (f32[624,768]{1,0:T(8,128)S(1)}, f32[624,768]{1,0:T(8,128)}, u32[]{:S(2)}) copy-start(f32[624,768]{1,0:T(8,128)} %get-tuple-element.25) | copy-start | bytes 5750788
  63.6 49.8 %collective-permute-start.7 = (bf16[2,2,208,768]{3,2,1,0:T(8,128)(2,1)}, bf16[2,2,208,768]{3,2,1,0:T(8,128)(2,1)}, u32[]{:S(2)}, u32[]{:S(2)}) collective-permute-start(bf16[2,2,208,768]{3,2,1,0:T(8,128)(2,1)} %slice.35), channel_id=1, source_target_pairs={{4,0},{8,4},{12,8},{5,1},{9,5},{13,9},{6,2},{10,6},{14,10},{7,3},{... | collective-permute-start | bytes 3833864 | tf_op jit(solution)/shard_map/ppermute | solution.py:20
  65.7 47.7 %collective-permute-start.4 = (bf16[2,2,208,768]{3,2,1,0:T(8,128)(2,1)}, bf16[2,2,208,768]{3,2,1,0:T(8,128)(2,1)}, u32[]{:S(2)}, u32[]{:S(2)}) collective-permute-start(bf16[2,2,208,768]{3,2,1,0:T(8,128)(2,1)} %slice.35), channel_id=1, source_target_pairs={{0,4},{4,8},{8,12},{1,5},{5,9},{9,13},{2,6},{6,10},{10,14},{3,7},{... | collective-permute-start | bytes 3833864 | tf_op jit(solution)/shard_map/ppermute | solution.py:20
  70.1 6.8 %copy-start.4 = (bf16[624,768]{1,0:T(8,128)(2,1)S(1)}, bf16[624,768]{1,0:T(8,128)(2,1)}, u32[]{:S(2)}) copy-start(bf16[624,768]{1,0:T(8,128)(2,1)} %copy-done.3) | copy-start | bytes 2875396
  72.2 41.2 %collective-permute-start.9 = (bf16[2,1,208,768]{3,2,1,0:T(8,128)(2,1)}, bf16[2,1,208,768]{3,2,1,0:T(8,128)(2,1)}, u32[]{:S(2)}, u32[]{:S(2)}) collective-permute-start(bf16[2,1,208,768]{3,2,1,0:T(8,128)(2,1)} %slice.37), channel_id=1, source_target_pairs={{0,2},{1,3},{4,6},{5,7},{8,10},{9,11},{12,14},{13,15},{16,18},{17,... | collective-permute-start | bytes 1916936 | tf_op jit(solution)/shard_map/ppermute | solution.py:20
  75.4 38.0 %collective-permute-start.6 = (bf16[2,1,208,768]{3,2,1,0:T(8,128)(2,1)}, bf16[2,1,208,768]{3,2,1,0:T(8,128)(2,1)}, u32[]{:S(2)}, u32[]{:S(2)}) collective-permute-start(bf16[2,1,208,768]{3,2,1,0:T(8,128)(2,1)} %slice.36), channel_id=1, source_target_pairs={{0,2},{1,3},{4,6},{5,7},{8,10},{9,11},{12,14},{13,15},{16,18},{17,... | collective-permute-start | bytes 1916936 | tf_op jit(solution)/shard_map/ppermute | solution.py:20
  143.8 4.3 %collective-permute-start.10 = (bf16[624,768]{1,0:T(8,128)(2,1)}, bf16[624,768]{1,0:T(8,128)(2,1)S(1)}, u32[]{:S(2)}, u32[]{:S(2)}) collective-permute-start(bf16[624,768]{1,0:T(8,128)(2,1)} %shard_map.119), channel_id=1, source_target_pairs={{0,1},{1,0},{2,3},{3,2},{4,5},{5,4},{6,7},{7,6},{8,9},{9,8},{10,11... | collective-permute-start | bytes 2875400 | tf_op jit(solution)/shard_map/ppermute | solution.py:57
  145.8 4.5 %copy-start.2 = (bf16[624,768]{1,0:T(8,128)(2,1)S(1)}, bf16[624,768]{1,0:T(8,128)(2,1)}, u32[]{:S(2)}) copy-start(bf16[624,768]{1,0:T(8,128)(2,1)} %reshape.51) | copy-start | bytes 2875396
  145.8 4.5 %copy-start.7 = (bf16[624,768]{1,0:T(8,128)(2,1)S(1)}, bf16[624,768]{1,0:T(8,128)(2,1)}, u32[]{:S(2)}) copy-start(bf16[624,768]{1,0:T(8,128)(2,1)} %shard_map.119) | copy-start | bytes 2875396
  (3 other events, 5.7 us)

commit v2 on v1

--- a/solution.py
+++ b/solution.py
@@ -80,12 +80,12 @@
             for n in group:
                 s = (
                     lax.dot_general(
-                        q, kv_ref[0, order_ref[frame, n]], (((1,), (1,)), ((), ())),
+                        q, kv_ref[0, n], (((1,), (1,)), ((), ())),
                         preferred_element_type=jnp.float32,
                     )
                     * score_scale
                 )
-                s = jnp.where(n < count, s, -jnp.inf)
+                s = jnp.where(order_ref[frame, n] > 0, s, -jnp.inf)
                 s_scr[n] = s
                 m_scr[...] = jnp.maximum(m_scr[...], s)
 
@@ -107,7 +107,7 @@
                 e = jnp.exp(s_scr[n] - m)
                 l_scr[...] += e
                 acc_scr[...] += jnp.dot(
-                    e.astype(jnp.bfloat16), kv_ref[1, order_ref[frame, n]],
+                    e.astype(jnp.bfloat16), kv_ref[1, n],
                     preferred_element_type=jnp.float32,
                 )
 
@@ -130,7 +130,7 @@
     n_tiles = len(slots)
     kv_all = jnp.concatenate([kv for kv, _ in kv_list], axis=1)
     seen = visible[:, jnp.array(slots, jnp.int32)]
-    order = jnp.argsort(1 - seen, axis=1, stable=True).astype(jnp.int32)
+    order = seen.astype(jnp.int32)
     count = jnp.sum(seen, axis=1).astype(jnp.int32)
     has_in = carry is not None
     group_size = n_tiles

time: 157 us -> 156 us (level)
  transfers between devices with their start and end apart: 12 -> 12, of which waited for: 2 -> 3; matrix products, arithmetic and copies ran while one was open for 25% -> 20% of each run, Pallas kernels for 37% -> 36%
where the time goes in v2:
time: 156 us; the launch traced here: 154 us
  Pallas kernels  56.2 us (36%)
  waiting for transfers between devices  30.1 us (19%)
  starting transfers between devices  18.5 us (12%)
  other arithmetic  17.7 us (11%)
  local copies, waits for them, and re-layouts  17.6 us (11%)
  matrix products  13 us (8%)
    pallas_call x2, Pallas kernels, attention(): pl.pallas_call(kernel, grid_spec=grid_spec, out_shape=out_shape, cost_est...  56.2 us
    ppermute x7, waiting for transfers between devices, from_behind(): lax.ppermute(value, axis, [(source, source + steps) for source in range(f...  27.2 us
    ppermute x7, starting transfers between devices, from_behind(): lax.ppermute(value, axis, [(source, source + steps) for source in range(f...  14.7 us
    concatenate x2, other arithmetic, attention(): kv_all = jnp.concatenate([kv for kv, _ in kv_list], axis=1)  10 us
    dot_general x1, matrix products, shards(): jnp.dot(hidden, query_weight, preferred_element_type=jnp.float32)  5.21 us
  transfers between devices with their start and end apart: 12, of which 3 were waited for; matrix products, arithmetic and copies ran while one was open for 20% of the time, Pallas kernels for 36%

profile of v2, /device:TPU:11, one launch (start us, length us, event | category | flops | bytes accessed | tf_op | source)
XLA Modules:
  0.0 154.0 jit_solution(9875098527491516278)
XLA Ops:
  0.0 1.4 copy.21
  5.7 1.6 %broadcast_select_fusion.1 = (bf16[624,768]{1,0:T(8,128)(2,1)S(1)}, bf16[624,768]{1,0:T(8,128)(2,1)S(1)}) fusion(bf16[624,768]{1,0:T(8,128)(2,1)} %reshape.51, bf16[624,768]{1,0:T(8,128)(2,1)} %collective-permute-done, pred[]{:T(512)S(6)} %eq.14), kind=kLoop, calls=%fused_computation.23 | loop fusion | flops 958464 | bytes 3833857 | tf_op jit(solution)/shard_map/jit(_where)/select_n | solution.py:28
  10.0 1.8 %multiply_reduce_fusion = (f32[624]{0:T(1024)S(1)}, f32[624,768]{1,0:T(8,128)S(1)}) fusion(bf16[624,1536]{1,0:T(8,128)(2,1)S(1)} %fusion.5, bf16[1536,768]{1,0:T(8,128)(2,1)S(1)} %copy-done.12), kind=kOutput, calls=%fused_computation.16 | convolution fusion | flops 1473158528 | bytes 6195648 | tf_op jit(solution)/shard_map/dot_general | solution.py:204
  12.4 1.6 %convolution_convert_fusion = bf16[624,768]{1,0:T(8,128)(2,1)S(1)} fusion(bf16[624,1536]{1,0:T(8,128)(2,1)S(1)} %fusion.5, bf16[1536,768]{1,0:T(8,128)(2,1)S(1)} %copy-done.13), kind=kOutput, calls=%fused_computation.19 | convolution fusion | flops 1472679936 | bytes 5234688 | tf_op jit(solution)/shard_map/dot_general | solution.py:205
  14.3 1.5 pad_maximum_fusion.3
  15.8 1.4 collective-permute-start.3
  17.2 2.1 %collective-permute-start.8 = (bf16[2,3,208,768]{3,2,1,0:T(8,128)(2,1)}, bf16[2,3,208,768]{3,2,1,0:T(8,128)(2,1)}, u32[]{:S(2)}, u32[]{:S(2)}) collective-permute-start(bf16[2,3,208,768]{3,2,1,0:T(8,128)(2,1)} %pad_maximum_fusion.3), channel_id=1, source_target_pairs={{4,0},{8,4},{12,8},{5,1},{9,5},{13,9},{6,2},{10,6},{14,10},{7,3},{... | collective-permute-start | bytes 5750792 | tf_op jit(solution)/shard_map/ppermute | solution.py:20
  19.3 3.2 %collective-permute-start.5 = (bf16[2,3,208,768]{3,2,1,0:T(8,128)(2,1)}, bf16[2,3,208,768]{3,2,1,0:T(8,128)(2,1)}, u32[]{:S(2)}, u32[]{:S(2)}) collective-permute-start(bf16[2,3,208,768]{3,2,1,0:T(8,128)(2,1)} %pad_maximum_fusion.3), channel_id=1, source_target_pairs={{0,4},{4,8},{8,12},{1,5},{5,9},{9,13},{2,6},{6,10},{10,14},{3,7},{... | collective-permute-start | bytes 5750792 | tf_op jit(solution)/shard_map/ppermute | solution.py:20
  25.0 5.2 %multiply_reduce_fusion.1 = (f32[624]{0:T(1024)S(1)}, f32[624,768]{1,0:T(8,128)}) fusion(bf16[624,1536]{1,0:T(8,128)(2,1)} %copy-done.5, bf16[1536,768]{1,0:T(8,128)(2,1)} %param.13), kind=kOutput, calls=%fused_computation.18 | convolution fusion | flops 1473158528 | bytes 6195648 | tf_op jit(solution)/shard_map/dot_general | solution.py:203
  33.9 27.2 %collective-permute-done.3 = bf16[2,3,208,768]{3,2,1,0:T(8,128)(2,1)} collective-permute-done((bf16[2,3,208,768]{3,2,1,0:T(8,128)(2,1)}, bf16[2,3,208,768]{3,2,1,0:T(8,128)(2,1)}, u32[]{:S(2)}, u32[]{:S(2)}) %collective-permute-start.3) | collective-permute-done | bytes 1916960 | tf_op jit(solution)/shard_map/ppermute | solution.py:20
  61.1 2.4 %slice.35 = bf16[2,2,208,768]{3,2,1,0:T(8,128)(2,1)} slice(bf16[2,3,208,768]{3,2,1,0:T(8,128)(2,1)} %collective-permute-done.3), slice={[0:2], [0:2], [0:208], [0:768]} | slice | bytes 2555904 | tf_op jit(solution)/shard_map/slice | solution.py:226
  63.5 2.1 %collective-permute-start.7 = (bf16[2,2,208,768]{3,2,1,0:T(8,128)(2,1)}, bf16[2,2,208,768]{3,2,1,0:T(8,128)(2,1)}, u32[]{:S(2)}, u32[]{:S(2)}) collective-permute-start(bf16[2,2,208,768]{3,2,1,0:T(8,128)(2,1)} %slice.35), channel_id=1, source_target_pairs={{4,0},{8,4},{12,8},{5,1},{9,5},{13,9},{6,2},{10,6},{14,10},{7,3},{... | collective-permute-start | bytes 3833864 | tf_op jit(solution)/shard_map/ppermute | solution.py:20
  65.6 3.2 %collective-permute-start.4 = (bf16[2,2,208,768]{3,2,1,0:T(8,128)(2,1)}, bf16[2,2,208,768]{3,2,1,0:T(8,128)(2,1)}, u32[]{:S(2)}, u32[]{:S(2)}) collective-permute-start(bf16[2,2,208,768]{3,2,1,0:T(8,128)(2,1)} %slice.35), channel_id=1, source_target_pairs={{0,4},{4,8},{8,12},{1,5},{5,9},{9,13},{2,6},{6,10},{10,14},{3,7},{... | collective-permute-start | bytes 3833864 | tf_op jit(solution)/shard_map/ppermute | solution.py:20
  70.0 2.1 %slice.37 = bf16[2,1,208,768]{3,2,1,0:T(8,128)(2,1)} slice(bf16[2,3,208,768]{3,2,1,0:T(8,128)(2,1)} %collective-permute-done.8), slice={[0:2], [2:3], [0:208], [0:768]} | slice | bytes 1277952 | tf_op jit(solution)/shard_map/slice | solution.py:229
  73.4 2.0 %slice.36 = bf16[2,1,208,768]{3,2,1,0:T(8,128)(2,1)} slice(bf16[2,3,208,768]{3,2,1,0:T(8,128)(2,1)} %collective-permute-done.5), slice={[0:2], [2:3], [0:208], [0:768]} | slice | bytes 1277952 | tf_op jit(solution)/shard_map/slice | solution.py:228
  75.3 1.5 collective-permute-start.6
  76.8 6.5 %pad_maximum_fusion.refs_0_ = bf16[2,12,208,768]{3,2,1,0:T(8,128)(2,1)} fusion(bf16[2,3,208,768]{3,2,1,0:T(8,128)(2,1)} %collective-permute-done.8, bf16[1,3,208,768]{3,2,1,0:T(8,128)(2,1)S(1)} %bitcast.32, bf16[1,3,208,768]{3,2,1,0:T(8,128)(2,1)S(1)} %bitcast.30, bf16[2,3,208,768]{3,2,1,0:T(8,128)(2,1)} %collective-permute-done.5, ...), kind=kLoop, calls=%fused_computation.2 | loop fusion | flops 15335424 | bytes 15335424 | tf_op jit(solution)/shard_map/concatenate | solution.py:131
  83.3 29.7 %shard_map.118 = (f32[624,768]{1,0:T(8,128)}, f32[624,768]{1,0:T(8,128)}, f32[624,768]{1,0:T(8,128)}) custom-call(s32[3,12]{1,0:T(4,128)} %bitcast.37, s32[3]{0:T(128)} %reduce_sum.59.count_ref, bf16[624,768]{1,0:T(8,128)(2,1)} %multiply_convert_fusion.1.q_ref, bf16[2,12,208,768]{3,2,1,0:T(8,128)(2,1)} %pad_maximum_fusion.refs_0_), custom_call_target="tpu_custom_call" | custom-call | flops 2392326144 | bytes 11501568 | tf_op jit(solution)/shard_map/pallas_call | solution.py:168
  113.0 3.5 %pad_maximum_fusion.1.refs_0_ = bf16[2,6,208,768]{3,2,1,0:T(8,128)(2,1)} fusion(bf16[2,1,208,768]{3,2,1,0:T(8,128)(2,1)} %collective-permute-done.9, bf16[2,2,208,768]{3,2,1,0:T(8,128)(2,1)} %collective-permute-done.7, bf16[2,1,208,768]{3,2,1,0:T(8,128)(2,1)} %collective-permute-done.6, bf16[2,2,208,768]{3,2,1,0:T(8,128)(2,1)} %collective-permute-done.4), kind=kLoop, calls=%fused_computation.11 | loop fusion | flops 5750784 | bytes 7667712 | tf_op jit(solution)/shard_map/concatenate | solution.py:131
  116.6 26.5 %shard_map.119 = bf16[624,768]{1,0:T(8,128)(2,1)} custom-call(s32[3,6]{1,0:T(4,128)} %bitcast.36, s32[3]{0:T(128)} %reduce_sum.54.count_ref, bf16[624,768]{1,0:T(8,128)(2,1)} %multiply_convert_fusion.1.q_ref, bf16[2,6,208,768]{3,2,1,0:T(8,128)(2,1)} %pad_maximum_fusion.1.refs_0_, f32[624,768]{1,0:T(8,128)} %get-tuple-element.8.refs_1_, ...), custom_call_target="tpu_custom_call" | custom-call | flops 1196163072 | bytes 7667712 | tf_op jit(solution)/shard_map/pallas_call | solution.py:168
  143.1 1.8 %collective-permute-start.10 = (bf16[624,768]{1,0:T(8,128)(2,1)}, bf16[624,768]{1,0:T(8,128)(2,1)S(1)}, u32[]{:S(2)}, u32[]{:S(2)}) collective-permute-start(bf16[624,768]{1,0:T(8,128)(2,1)} %shard_map.119), channel_id=1, source_target_pairs={{0,1},{1,0},{2,3},{3,2},{4,5},{5,4},{6,7},{7,6},{8,9},{9,8},{10,11... | collective-permute-start | bytes 2875400 | tf_op jit(solution)/shard_map/ppermute | solution.py:57
  144.9 2.3 %collective-permute-done.10 = bf16[624,768]{1,0:T(8,128)(2,1)S(1)} collective-permute-done((bf16[624,768]{1,0:T(8,128)(2,1)}, bf16[624,768]{1,0:T(8,128)(2,1)S(1)}, u32[]{:S(2)}, u32[]{:S(2)}) %collective-permute-start.10) | collective-permute-done | bytes 958496 | tf_op jit(solution)/shard_map/ppermute | solution.py:57
  147.2 2.2 %fusion.13 = f32[624,768]{1,0:T(8,128)S(1)} fusion(bf16[624,768]{1,0:T(8,128)(2,1)S(1)} %collective-permute-done.10, bf16[768,768]{1,0:T(8,128)(2,1)} %collective-permute-done.11), kind=kOutput, calls=%fused_computation.42 | convolution fusion | flops 736100352 | bytes 4055040 | tf_op jit(solution)/shard_map/dot_general | solution.py:58
  149.4 1.9 %add_convert_fusion = bf16[624,768]{1,0:T(8,128)(2,1)} fusion(f32[624,768]{1,0:T(8,128)S(1)} %fusion.13, bf16[624,768]{1,0:T(8,128)(2,1)S(1)} %copy-done.1, bf16[624,768]{1,0:T(8,128)(2,1)S(1)} %copy-done.6, bf16[768,1536]{1,0:T(8,128)(2,1)S(1)} %copy-done, s32[]{:T(128)S(6)} %select_n.25, f32[768]{0:T(1024)S(1)} %dynamic_slice.9), kind=kOutput, calls=%fused_computation.14 | convolution fusion | flops 738496512 | bytes 5976068 | tf_op jit(solution)/shard_map/dot_general | solution.py:58
  (75 shorter events, 18.4 us)
Async XLA Ops:
  0.0 22.5 %copy-start = (bf16[768,1536]{1,0:T(8,128)(2,1)S(1)}, bf16[768,1536]{1,0:T(8,128)(2,1)}, u32[]{:S(2)}) copy-start(bf16[768,1536]{1,0:T(8,128)(2,1)} %param.16) | copy-start | bytes 7077892
  2.6 3.2 %collective-permute-start = (bf16[624,768]{1,0:T(8,128)(2,1)}, bf16[624,768]{1,0:T(8,128)(2,1)}, u32[]{:S(2)}, u32[]{:S(2)}) collective-permute-start(bf16[624,768]{1,0:T(8,128)(2,1)} %reshape.51), channel_id=1, source_target_pairs={{0,1},{1,0},{2,3},{3,2},{4,5},{5,4},{6,7},{7,6},{8,9},{9,8},{10,11... | collective-permute-start | bytes 2875400 | tf_op jit(solution)/shard_map/ppermute | solution.py:27
  10.0 2.2 %copy-start.5 = (bf16[624,1536]{1,0:T(8,128)(2,1)}, bf16[624,1536]{1,0:T(8,128)(2,1)S(1)}, u32[]{:S(2)}) copy-start(bf16[624,1536]{1,0:T(8,128)(2,1)S(1)} %fusion.5) | copy-start | bytes 5750788
  10.0 2.4 %copy-start.13 = (bf16[1536,768]{1,0:T(8,128)(2,1)S(1)}, bf16[1536,768]{1,0:T(8,128)(2,1)}, u32[]{:S(2)}) copy-start(bf16[1536,768]{1,0:T(8,128)(2,1)} %param.15) | copy-start | bytes 7077892
  11.8 2.3 %copy-start.8 = (f32[768]{0:T(1024)S(1)}, f32[768]{0:T(1024)}, u32[]{:S(2)}) copy-start(f32[768]{0:T(1024)} %param.18) | copy-start | bytes 9220
  11.8 2.3 %collective-permute-start.2 = (f32[624]{0:T(1024)S(1)}, f32[624]{0:T(1024)S(1)}, u32[]{:S(2)}, u32[]{:S(2)}) collective-permute-start(f32[624]{0:T(1024)S(1)} %get-tuple-element.18), channel_id=1, source_target_pairs={{0,1},{1,0},{2,3},{3,2},{4,5},{5,4},{6,7},{7,6},{8,9},{9,8},{10,11... | collective-permute-start | bytes 7496 | tf_op jit(solution)/shard_map/ppermute | solution.py:45
  15.8 8.8 %copy-start.7 = (s32[1,3,6,3]{2,0,3,1:T(1,128)S(1)}, s32[1,3,6,3]{2,0,3,1:T(1,128)}, u32[]{:S(2)}) copy-start(s32[1,3,6,3]{2,0,3,1:T(1,128)} %param.21) | copy-start | bytes 652
  15.8 9.1 %copy-start.11 = (s32[6]{0:T(128)S(1)}, s32[6]{0:T(128)}, u32[]{:S(2)}) copy-start(s32[6]{0:T(128)} %constant.61) | copy-start | bytes 76
  15.8 45.3 %collective-permute-start.3 = (bf16[2,3,208,768]{3,2,1,0:T(8,128)(2,1)}, bf16[2,3,208,768]{3,2,1,0:T(8,128)(2,1)}, u32[]{:S(2)}, u32[]{:S(2)}) collective-permute-start(bf16[2,3,208,768]{3,2,1,0:T(8,128)(2,1)} %pad_maximum_fusion.3), channel_id=1, source_target_pairs={{0,2},{1,3},{4,6},{5,7},{8,10},{9,11},{12,14},{13,15},{16,18},{17,... | collective-permute-start | bytes 5750792 | tf_op jit(solution)/shard_map/ppermute | solution.py:20
  17.2 52.8 %collective-permute-start.8 = (bf16[2,3,208,768]{3,2,1,0:T(8,128)(2,1)}, bf16[2,3,208,768]{3,2,1,0:T(8,128)(2,1)}, u32[]{:S(2)}, u32[]{:S(2)}) collective-permute-start(bf16[2,3,208,768]{3,2,1,0:T(8,128)(2,1)} %pad_maximum_fusion.3), channel_id=1, source_target_pairs={{4,0},{8,4},{12,8},{5,1},{9,5},{13,9},{6,2},{10,6},{14,10},{7,3},{... | collective-permute-start | bytes 5750792 | tf_op jit(solution)/shard_map/ppermute | solution.py:20
  19.3 54.0 %collective-permute-start.5 = (bf16[2,3,208,768]{3,2,1,0:T(8,128)(2,1)}, bf16[2,3,208,768]{3,2,1,0:T(8,128)(2,1)}, u32[]{:S(2)}, u32[]{:S(2)}) collective-permute-start(bf16[2,3,208,768]{3,2,1,0:T(8,128)(2,1)} %pad_maximum_fusion.3), channel_id=1, source_target_pairs={{0,4},{4,8},{8,12},{1,5},{5,9},{9,13},{2,6},{6,10},{10,14},{3,7},{... | collective-permute-start | bytes 5750792 | tf_op jit(solution)/shard_map/ppermute | solution.py:20
  23.7 121.3 %collective-permute-start.11 = (bf16[768,768]{1,0:T(8,128)(2,1)}, bf16[768,768]{1,0:T(8,128)(2,1)}, u32[]{:S(2)}, u32[]{:S(2)}) collective-permute-start(bf16[768,768]{1,0:T(8,128)(2,1)} %constant_dynamic-slice_fusion), channel_id=1, source_target_pairs={{0,1},{1,0},{2,3},{3,2},{4,5},{5,4},{6,7},{7,6},{8,9},{9,8},{10,11... | collective-permute-start | bytes 3538952 | tf_op jit(solution)/shard_map/ppermute | solution.py:56
  25.0 5.2 %copy-start.10 = (s32[12]{0:T(128)S(1)}, s32[12]{0:T(128)}, u32[]{:S(2)}) copy-start(s32[12]{0:T(128)} %constant.62) | copy-start | bytes 148
  30.2 38.6 %copy-start.9 = (f32[768]{0:T(1024)S(1)}, f32[768]{0:T(1024)}, u32[]{:S(2)}) copy-start(f32[768]{0:T(1024)} %param.17) | copy-start | bytes 9220
  30.2 3.7 %collective-permute-start.1 = (f32[624]{0:T(1024)S(1)}, f32[624]{0:T(1024)S(1)}, u32[]{:S(2)}, u32[]{:S(2)}) collective-permute-start(f32[624]{0:T(1024)S(1)} %get-tuple-element.16), channel_id=1, source_target_pairs={{0,1},{1,0},{2,3},{3,2},{4,5},{5,4},{6,7},{7,6},{8,9},{9,8},{10,11... | collective-permute-start | bytes 7496 | tf_op jit(solution)/shard_map/ppermute | solution.py:45
  33.9 34.9 %copy-start.4 = (f32[624,768]{1,0:T(8,128)S(1)}, f32[624,768]{1,0:T(8,128)}, u32[]{:S(2)}) copy-start(f32[624,768]{1,0:T(8,128)} %get-tuple-element.17) | copy-start | bytes 5750788
  63.5 49.5 %collective-permute-start.7 = (bf16[2,2,208,768]{3,2,1,0:T(8,128)(2,1)}, bf16[2,2,208,768]{3,2,1,0:T(8,128)(2,1)}, u32[]{:S(2)}, u32[]{:S(2)}) collective-permute-start(bf16[2,2,208,768]{3,2,1,0:T(8,128)(2,1)} %slice.35), channel_id=1, source_target_pairs={{4,0},{8,4},{12,8},{5,1},{9,5},{13,9},{6,2},{10,6},{14,10},{7,3},{... | collective-permute-start | bytes 3833864 | tf_op jit(solution)/shard_map/ppermute | solution.py:20
  65.6 47.4 %collective-permute-start.4 = (bf16[2,2,208,768]{3,2,1,0:T(8,128)(2,1)}, bf16[2,2,208,768]{3,2,1,0:T(8,128)(2,1)}, u32[]{:S(2)}, u32[]{:S(2)}) collective-permute-start(bf16[2,2,208,768]{3,2,1,0:T(8,128)(2,1)} %slice.35), channel_id=1, source_target_pairs={{0,4},{4,8},{8,12},{1,5},{5,9},{9,13},{2,6},{6,10},{10,14},{3,7},{... | collective-permute-start | bytes 3833864 | tf_op jit(solution)/shard_map/ppermute | solution.py:20
  70.0 6.8 %copy-start.3 = (bf16[624,768]{1,0:T(8,128)(2,1)S(1)}, bf16[624,768]{1,0:T(8,128)(2,1)}, u32[]{:S(2)}) copy-start(bf16[624,768]{1,0:T(8,128)(2,1)} %copy-done.2) | copy-start | bytes 2875396
  72.1 40.9 %collective-permute-start.9 = (bf16[2,1,208,768]{3,2,1,0:T(8,128)(2,1)}, bf16[2,1,208,768]{3,2,1,0:T(8,128)(2,1)}, u32[]{:S(2)}, u32[]{:S(2)}) collective-permute-start(bf16[2,1,208,768]{3,2,1,0:T(8,128)(2,1)} %slice.37), channel_id=1, source_target_pairs={{0,2},{1,3},{4,6},{5,7},{8,10},{9,11},{12,14},{13,15},{16,18},{17,... | collective-permute-start | bytes 1916936 | tf_op jit(solution)/shard_map/ppermute | solution.py:20
  75.3 37.7 %collective-permute-start.6 = (bf16[2,1,208,768]{3,2,1,0:T(8,128)(2,1)}, bf16[2,1,208,768]{3,2,1,0:T(8,128)(2,1)}, u32[]{:S(2)}, u32[]{:S(2)}) collective-permute-start(bf16[2,1,208,768]{3,2,1,0:T(8,128)(2,1)} %slice.36), channel_id=1, source_target_pairs={{0,2},{1,3},{4,6},{5,7},{8,10},{9,11},{12,14},{13,15},{16,18},{17,... | collective-permute-start | bytes 1916936 | tf_op jit(solution)/shard_map/ppermute | solution.py:20
  143.1 4.1 %collective-permute-start.10 = (bf16[624,768]{1,0:T(8,128)(2,1)}, bf16[624,768]{1,0:T(8,128)(2,1)S(1)}, u32[]{:S(2)}, u32[]{:S(2)}) collective-permute-start(bf16[624,768]{1,0:T(8,128)(2,1)} %shard_map.119), channel_id=1, source_target_pairs={{0,1},{1,0},{2,3},{3,2},{4,5},{5,4},{6,7},{7,6},{8,9},{9,8},{10,11... | collective-permute-start | bytes 2875400 | tf_op jit(solution)/shard_map/ppermute | solution.py:57
  144.9 4.5 %copy-start.1 = (bf16[624,768]{1,0:T(8,128)(2,1)S(1)}, bf16[624,768]{1,0:T(8,128)(2,1)}, u32[]{:S(2)}) copy-start(bf16[624,768]{1,0:T(8,128)(2,1)} %reshape.51) | copy-start | bytes 2875396
  144.9 4.5 %copy-start.6 = (bf16[624,768]{1,0:T(8,128)(2,1)S(1)}, bf16[624,768]{1,0:T(8,128)(2,1)}, u32[]{:S(2)}) copy-start(bf16[624,768]{1,0:T(8,128)(2,1)} %shard_map.119) | copy-start | bytes 2875396
  (2 other events, 3.4 us)

commit v3 on v2

--- a/solution.py
+++ b/solution.py
@@ -61,6 +61,10 @@
 
 
 GROUP = 3
+
+
+def run_now(body):
+    return body()
 
 
 def attention_kernel(score_scale, n_tiles, group_size, has_in, has_out, order_ref, count_ref, q_ref, *refs):
@@ -75,7 +79,7 @@
     m_scr[...] = jnp.full(m_scr.shape, -jnp.inf, jnp.float32)
     for group in groups:
 
-        @pl.when(count > group[0])
+        @run_now
         def _():
             for n in group:
                 s = (
@@ -101,7 +105,7 @@
     l_scr[...] = jnp.zeros(l_scr.shape, jnp.float32)
     for group in groups:
 
-        @pl.when(count > group[0])
+        @run_now
         def _():
             for n in group:
                 e = jnp.exp(s_scr[n] - m)

time: 156 us -> 170 us (1.090)
  the two profiles are of different devices: /device:TPU:11 before, /device:TPU:0 now
where the time goes in v3:
time: 170 us; the launch traced here: 169 us
  Pallas kernels  65.6 us (39%)
  starting transfers between devices  29 us (17%)
  waiting for transfers between devices  25.5 us (15%)
  local copies, waits for them, and re-layouts  17.6 us (10%)
  other arithmetic  17.6 us (10%)
  matrix products  13 us (8%)
    pallas_call x2, Pallas kernels, attention(): pl.pallas_call(kernel, grid_spec=grid_spec, out_shape=out_shape, cost_est...  65.6 us
    ppermute x7, starting transfers between devices, from_behind(): lax.ppermute(value, axis, [(source, source + steps) for source in range(f...  27.6 us
    ppermute x7, waiting for transfers between devices, from_behind(): lax.ppermute(value, axis, [(source, source + steps) for source in range(f...  22.2 us
    concatenate x2, other arithmetic, attention(): kv_all = jnp.concatenate([kv for kv, _ in kv_list], axis=1)  10 us
    dot_general x1, matrix products, shards(): jnp.dot(hidden, query_weight, preferred_element_type=jnp.float32)  5.21 us
  transfers between devices with their start and end apart: 12, of which 3 were waited for; matrix products, arithmetic and copies ran while one was open for 18% of the time, Pallas kernels for 39%

profile of v3, /device:TPU:0, one launch (start us, length us, event | category | flops | bytes accessed | tf_op | source)
XLA Modules:
  0.0 169.2 jit_solution(6727639241507061016)
XLA Ops:
  0.0 1.4 copy.21
  5.5 1.6 broadcast_select_fusion.1
  9.8 1.8 %multiply_reduce_fusion = (f32[624]{0:T(1024)S(1)}, f32[624,768]{1,0:T(8,128)S(1)}) fusion(bf16[624,1536]{1,0:T(8,128)(2,1)S(1)} %fusion.5, bf16[1536,768]{1,0:T(8,128)(2,1)S(1)} %copy-done.12), kind=kOutput, calls=%fused_computation.16 | convolution fusion | flops 1473158528 | bytes 6195648 | tf_op jit(solution)/shard_map/dot_general | solution.py:208
  12.2 1.6 convolution_convert_fusion
  14.1 1.5 pad_maximum_fusion.3
  15.6 6.2 %collective-permute-start.3 = (bf16[2,3,208,768]{3,2,1,0:T(8,128)(2,1)}, bf16[2,3,208,768]{3,2,1,0:T(8,128)(2,1)}, u32[]{:S(2)}, u32[]{:S(2)}) collective-permute-start(bf16[2,3,208,768]{3,2,1,0:T(8,128)(2,1)} %pad_maximum_fusion.3), channel_id=1, source_target_pairs={{0,2},{1,3},{4,6},{5,7},{8,10},{9,11},{12,14},{13,15},{16,18},{17,... | collective-permute-start | bytes 5750792 | tf_op jit(solution)/shard_map/ppermute | solution.py:20
  23.0 5.9 %collective-permute-start.5 = (bf16[2,3,208,768]{3,2,1,0:T(8,128)(2,1)}, bf16[2,3,208,768]{3,2,1,0:T(8,128)(2,1)}, u32[]{:S(2)}, u32[]{:S(2)}) collective-permute-start(bf16[2,3,208,768]{3,2,1,0:T(8,128)(2,1)} %pad_maximum_fusion.3), channel_id=1, source_target_pairs={{0,4},{4,8},{8,12},{1,5},{5,9},{9,13},{2,6},{6,10},{10,14},{3,7},{... | collective-permute-start | bytes 5750792 | tf_op jit(solution)/shard_map/ppermute | solution.py:20
  30.4 5.2 %multiply_reduce_fusion.1 = (f32[624]{0:T(1024)S(1)}, f32[624,768]{1,0:T(8,128)}) fusion(bf16[624,1536]{1,0:T(8,128)(2,1)} %copy-done.5, bf16[1536,768]{1,0:T(8,128)(2,1)} %param.13), kind=kOutput, calls=%fused_computation.18 | convolution fusion | flops 1473158528 | bytes 6195648 | tf_op jit(solution)/shard_map/dot_general | solution.py:207
  39.9 22.2 %collective-permute-done.3 = bf16[2,3,208,768]{3,2,1,0:T(8,128)(2,1)} collective-permute-done((bf16[2,3,208,768]{3,2,1,0:T(8,128)(2,1)}, bf16[2,3,208,768]{3,2,1,0:T(8,128)(2,1)}, u32[]{:S(2)}, u32[]{:S(2)}) %collective-permute-start.3) | collective-permute-done | bytes 1916960 | tf_op jit(solution)/shard_map/ppermute | solution.py:20
  62.1 2.4 %slice.35 = bf16[2,2,208,768]{3,2,1,0:T(8,128)(2,1)} slice(bf16[2,3,208,768]{3,2,1,0:T(8,128)(2,1)} %collective-permute-done.3), slice={[0:2], [0:2], [0:208], [0:768]} | slice | bytes 2555904 | tf_op jit(solution)/shard_map/slice | solution.py:230
  65.8 5.6 %collective-permute-start.4 = (bf16[2,2,208,768]{3,2,1,0:T(8,128)(2,1)}, bf16[2,2,208,768]{3,2,1,0:T(8,128)(2,1)}, u32[]{:S(2)}, u32[]{:S(2)}) collective-permute-start(bf16[2,2,208,768]{3,2,1,0:T(8,128)(2,1)} %slice.35), channel_id=1, source_target_pairs={{0,4},{4,8},{8,12},{1,5},{5,9},{9,13},{2,6},{6,10},{10,14},{3,7},{... | collective-permute-start | bytes 3833864 | tf_op jit(solution)/shard_map/ppermute | solution.py:20
  72.6 2.1 %slice.37 = bf16[2,1,208,768]{3,2,1,0:T(8,128)(2,1)} slice(bf16[2,3,208,768]{3,2,1,0:T(8,128)(2,1)} %collective-permute-done.8), slice={[0:2], [2:3], [0:208], [0:768]} | slice | bytes 1277952 | tf_op jit(solution)/shard_map/slice | solution.py:233
  74.7 5.2 %collective-permute-start.9 = (bf16[2,1,208,768]{3,2,1,0:T(8,128)(2,1)}, bf16[2,1,208,768]{3,2,1,0:T(8,128)(2,1)}, u32[]{:S(2)}, u32[]{:S(2)}) collective-permute-start(bf16[2,1,208,768]{3,2,1,0:T(8,128)(2,1)} %slice.37), channel_id=1, source_target_pairs={{0,2},{1,3},{4,6},{5,7},{8,10},{9,11},{12,14},{13,15},{16,18},{17,... | collective-permute-start | bytes 1916936 | tf_op jit(solution)/shard_map/ppermute | solution.py:20
  79.9 2.0 %slice.36 = bf16[2,1,208,768]{3,2,1,0:T(8,128)(2,1)} slice(bf16[2,3,208,768]{3,2,1,0:T(8,128)(2,1)} %collective-permute-done.5), slice={[0:2], [2:3], [0:208], [0:768]} | slice | bytes 1277952 | tf_op jit(solution)/shard_map/slice | solution.py:232
  81.9 2.1 %collective-permute-start.6 = (bf16[2,1,208,768]{3,2,1,0:T(8,128)(2,1)}, bf16[2,1,208,768]{3,2,1,0:T(8,128)(2,1)}, u32[]{:S(2)}, u32[]{:S(2)}) collective-permute-start(bf16[2,1,208,768]{3,2,1,0:T(8,128)(2,1)} %slice.36), channel_id=1, source_target_pairs={{0,2},{1,3},{4,6},{5,7},{8,10},{9,11},{12,14},{13,15},{16,18},{17,... | collective-permute-start | bytes 1916936 | tf_op jit(solution)/shard_map/ppermute | solution.py:20
  84.0 6.5 %pad_maximum_fusion.refs_0_ = bf16[2,12,208,768]{3,2,1,0:T(8,128)(2,1)} fusion(bf16[2,3,208,768]{3,2,1,0:T(8,128)(2,1)} %collective-permute-done.8, bf16[1,3,208,768]{3,2,1,0:T(8,128)(2,1)S(1)} %bitcast.32, bf16[1,3,208,768]{3,2,1,0:T(8,128)(2,1)S(1)} %bitcast.30, bf16[2,3,208,768]{3,2,1,0:T(8,128)(2,1)} %collective-permute-done.5, ...), kind=kLoop, calls=%fused_computation.2 | loop fusion | flops 15335424 | bytes 15335424 | tf_op jit(solution)/shard_map/concatenate | solution.py:135
  90.5 39.5 %shard_map.118 = (f32[624,768]{1,0:T(8,128)}, f32[624,768]{1,0:T(8,128)}, f32[624,768]{1,0:T(8,128)}) custom-call(s32[3,12]{1,0:T(4,128)} %bitcast.37, s32[3]{0:T(128)} %reduce_sum.59.count_ref, bf16[624,768]{1,0:T(8,128)(2,1)} %multiply_convert_fusion.1.q_ref, bf16[2,12,208,768]{3,2,1,0:T(8,128)(2,1)} %pad_maximum_fusion.refs_0_), custom_call_target="tpu_custom_call" | custom-call | flops 2392326144 | bytes 11501568 | tf_op jit(solution)/shard_map/pallas_call | solution.py:172
  130.1 3.5 %pad_maximum_fusion.1.refs_0_ = bf16[2,6,208,768]{3,2,1,0:T(8,128)(2,1)} fusion(bf16[2,1,208,768]{3,2,1,0:T(8,128)(2,1)} %collective-permute-done.9, bf16[2,2,208,768]{3,2,1,0:T(8,128)(2,1)} %collective-permute-done.7, bf16[2,1,208,768]{3,2,1,0:T(8,128)(2,1)} %collective-permute-done.6, bf16[2,2,208,768]{3,2,1,0:T(8,128)(2,1)} %collective-permute-done.4), kind=kLoop, calls=%fused_computation.11 | loop fusion | flops 5750784 | bytes 7667712 | tf_op jit(solution)/shard_map/concatenate | solution.py:135
  133.6 26.1 %shard_map.119 = bf16[624,768]{1,0:T(8,128)(2,1)} custom-call(s32[3,6]{1,0:T(4,128)} %bitcast.36, s32[3]{0:T(128)} %reduce_sum.54.count_ref, bf16[624,768]{1,0:T(8,128)(2,1)} %multiply_convert_fusion.1.q_ref, bf16[2,6,208,768]{3,2,1,0:T(8,128)(2,1)} %pad_maximum_fusion.1.refs_0_, f32[624,768]{1,0:T(8,128)} %get-tuple-element.8.refs_1_, ...), custom_call_target="tpu_custom_call" | custom-call | flops 1196163072 | bytes 7667712 | tf_op jit(solution)/shard_map/pallas_call | solution.py:172
  159.7 2.7 %collective-permute-done.10 = bf16[624,768]{1,0:T(8,128)(2,1)S(1)} collective-permute-done((bf16[624,768]{1,0:T(8,128)(2,1)}, bf16[624,768]{1,0:T(8,128)(2,1)S(1)}, u32[]{:S(2)}, u32[]{:S(2)}) %collective-permute-start.10) | collective-permute-done | bytes 958496 | tf_op jit(solution)/shard_map/ppermute | solution.py:57
  162.4 2.2 %fusion.13 = f32[624,768]{1,0:T(8,128)S(1)} fusion(bf16[624,768]{1,0:T(8,128)(2,1)S(1)} %collective-permute-done.10, bf16[768,768]{1,0:T(8,128)(2,1)} %collective-permute-done.11), kind=kOutput, calls=%fused_computation.42 | convolution fusion | flops 736100352 | bytes 4055040 | tf_op jit(solution)/shard_map/dot_general | solution.py:58
  164.6 1.9 %add_convert_fusion = bf16[624,768]{1,0:T(8,128)(2,1)} fusion(f32[624,768]{1,0:T(8,128)S(1)} %fusion.13, bf16[624,768]{1,0:T(8,128)(2,1)S(1)} %copy-done.1, bf16[624,768]{1,0:T(8,128)(2,1)S(1)} %copy-done.6, bf16[768,1536]{1,0:T(8,128)(2,1)S(1)} %copy-done, s32[]{:T(128)S(6)} %select_n.25, f32[768]{0:T(1024)S(1)} %dynamic_slice.9), kind=kOutput, calls=%fused_computation.14 | convolution fusion | flops 738496512 | bytes 5976068 | tf_op jit(solution)/shard_map/dot_general | solution.py:58
  166.5 1.3 reshape.53
  167.8 1.3 copy.29
  (75 shorter events, 16.4 us)
Async XLA Ops:
  0.0 28.9 %copy-start = (bf16[768,1536]{1,0:T(8,128)(2,1)S(1)}, bf16[768,1536]{1,0:T(8,128)(2,1)}, u32[]{:S(2)}) copy-start(bf16[768,1536]{1,0:T(8,128)(2,1)} %param.16) | copy-start | bytes 7077892
  2.6 3.0 %collective-permute-start = (bf16[624,768]{1,0:T(8,128)(2,1)}, bf16[624,768]{1,0:T(8,128)(2,1)}, u32[]{:S(2)}, u32[]{:S(2)}) collective-permute-start(bf16[624,768]{1,0:T(8,128)(2,1)} %reshape.51), channel_id=1, source_target_pairs={{0,1},{1,0},{2,3},{3,2},{4,5},{5,4},{6,7},{7,6},{8,9},{9,8},{10,11... | collective-permute-start | bytes 2875400 | tf_op jit(solution)/shard_map/ppermute | solution.py:27
  9.8 2.2 %copy-start.5 = (bf16[624,1536]{1,0:T(8,128)(2,1)}, bf16[624,1536]{1,0:T(8,128)(2,1)S(1)}, u32[]{:S(2)}) copy-start(bf16[624,1536]{1,0:T(8,128)(2,1)S(1)} %fusion.5) | copy-start | bytes 5750788
  9.8 2.4 %copy-start.13 = (bf16[1536,768]{1,0:T(8,128)(2,1)S(1)}, bf16[1536,768]{1,0:T(8,128)(2,1)}, u32[]{:S(2)}) copy-start(bf16[1536,768]{1,0:T(8,128)(2,1)} %param.15) | copy-start | bytes 7077892
  11.6 2.3 %copy-start.8 = (f32[768]{0:T(1024)S(1)}, f32[768]{0:T(1024)}, u32[]{:S(2)}) copy-start(f32[768]{0:T(1024)} %param.18) | copy-start | bytes 9220
  11.6 2.3 %collective-permute-start.2 = (f32[624]{0:T(1024)S(1)}, f32[624]{0:T(1024)S(1)}, u32[]{:S(2)}, u32[]{:S(2)}) collective-permute-start(f32[624]{0:T(1024)S(1)} %get-tuple-element.18), channel_id=1, source_target_pairs={{0,1},{1,0},{2,3},{3,2},{4,5},{5,4},{6,7},{7,6},{8,9},{9,8},{10,11... | collective-permute-start | bytes 7496 | tf_op jit(solution)/shard_map/ppermute | solution.py:45
  15.6 14.5 %copy-start.7 = (s32[1,3,6,3]{2,0,3,1:T(1,128)S(1)}, s32[1,3,6,3]{2,0,3,1:T(1,128)}, u32[]{:S(2)}) copy-start(s32[1,3,6,3]{2,0,3,1:T(1,128)} %param.21) | copy-start | bytes 652
  15.6 14.8 %copy-start.11 = (s32[6]{0:T(128)S(1)}, s32[6]{0:T(128)}, u32[]{:S(2)}) copy-start(s32[6]{0:T(128)} %constant.61) | copy-start | bytes 76
  15.6 46.5 %collective-permute-start.3 = (bf16[2,3,208,768]{3,2,1,0:T(8,128)(2,1)}, bf16[2,3,208,768]{3,2,1,0:T(8,128)(2,1)}, u32[]{:S(2)}, u32[]{:S(2)}) collective-permute-start(bf16[2,3,208,768]{3,2,1,0:T(8,128)(2,1)} %pad_maximum_fusion.3), channel_id=1, source_target_pairs={{0,2},{1,3},{4,6},{5,7},{8,10},{9,11},{12,14},{13,15},{16,18},{17,... | collective-permute-start | bytes 5750792 | tf_op jit(solution)/shard_map/ppermute | solution.py:20
  21.7 50.9 %collective-permute-start.8 = (bf16[2,3,208,768]{3,2,1,0:T(8,128)(2,1)}, bf16[2,3,208,768]{3,2,1,0:T(8,128)(2,1)}, u32[]{:S(2)}, u32[]{:S(2)}) collective-permute-start(bf16[2,3,208,768]{3,2,1,0:T(8,128)(2,1)} %pad_maximum_fusion.3), channel_id=1, source_target_pairs={{4,0},{8,4},{12,8},{5,1},{9,5},{13,9},{6,2},{10,6},{14,10},{7,3},{... | collective-permute-start | bytes 5750792 | tf_op jit(solution)/shard_map/ppermute | solution.py:20
  23.0 56.9 %collective-permute-start.5 = (bf16[2,3,208,768]{3,2,1,0:T(8,128)(2,1)}, bf16[2,3,208,768]{3,2,1,0:T(8,128)(2,1)}, u32[]{:S(2)}, u32[]{:S(2)}) collective-permute-start(bf16[2,3,208,768]{3,2,1,0:T(8,128)(2,1)} %pad_maximum_fusion.3), channel_id=1, source_target_pairs={{0,4},{4,8},{8,12},{1,5},{5,9},{9,13},{2,6},{6,10},{10,14},{3,7},{... | collective-permute-start | bytes 5750792 | tf_op jit(solution)/shard_map/ppermute | solution.py:20
  30.1 129.7 %collective-permute-start.11 = (bf16[768,768]{1,0:T(8,128)(2,1)}, bf16[768,768]{1,0:T(8,128)(2,1)}, u32[]{:S(2)}, u32[]{:S(2)}) collective-permute-start(bf16[768,768]{1,0:T(8,128)(2,1)} %constant_dynamic-slice_fusion), channel_id=1, source_target_pairs={{0,1},{1,0},{2,3},{3,2},{4,5},{5,4},{6,7},{7,6},{8,9},{9,8},{10,11... | collective-permute-start | bytes 3538952 | tf_op jit(solution)/shard_map/ppermute | solution.py:56
  30.4 5.7 %copy-start.10 = (s32[12]{0:T(128)S(1)}, s32[12]{0:T(128)}, u32[]{:S(2)}) copy-start(s32[12]{0:T(128)} %constant.62) | copy-start | bytes 148
  35.7 35.8 %copy-start.9 = (f32[768]{0:T(1024)S(1)}, f32[768]{0:T(1024)}, u32[]{:S(2)}) copy-start(f32[768]{0:T(1024)} %param.17) | copy-start | bytes 9220
  35.7 4.2 %collective-permute-start.1 = (f32[624]{0:T(1024)S(1)}, f32[624]{0:T(1024)S(1)}, u32[]{:S(2)}, u32[]{:S(2)}) collective-permute-start(f32[624]{0:T(1024)S(1)} %get-tuple-element.16), channel_id=1, source_target_pairs={{0,1},{1,0},{2,3},{3,2},{4,5},{5,4},{6,7},{7,6},{8,9},{9,8},{10,11... | collective-permute-start | bytes 7496 | tf_op jit(solution)/shard_map/ppermute | solution.py:45
  39.9 31.6 %copy-start.4 = (f32[624,768]{1,0:T(8,128)S(1)}, f32[624,768]{1,0:T(8,128)}, u32[]{:S(2)}) copy-start(f32[624,768]{1,0:T(8,128)} %get-tuple-element.17) | copy-start | bytes 5750788
  64.5 65.5 %collective-permute-start.7 = (bf16[2,2,208,768]{3,2,1,0:T(8,128)(2,1)}, bf16[2,2,208,768]{3,2,1,0:T(8,128)(2,1)}, u32[]{:S(2)}, u32[]{:S(2)}) collective-permute-start(bf16[2,2,208,768]{3,2,1,0:T(8,128)(2,1)} %slice.35), channel_id=1, source_target_pairs={{4,0},{8,4},{12,8},{5,1},{9,5},{13,9},{6,2},{10,6},{14,10},{7,3},{... | collective-permute-start | bytes 3833864 | tf_op jit(solution)/shard_map/ppermute | solution.py:20
  65.8 64.2 %collective-permute-start.4 = (bf16[2,2,208,768]{3,2,1,0:T(8,128)(2,1)}, bf16[2,2,208,768]{3,2,1,0:T(8,128)(2,1)}, u32[]{:S(2)}, u32[]{:S(2)}) collective-permute-start(bf16[2,2,208,768]{3,2,1,0:T(8,128)(2,1)} %slice.35), channel_id=1, source_target_pairs={{0,4},{4,8},{8,12},{1,5},{5,9},{9,13},{2,6},{6,10},{10,14},{3,7},{... | collective-permute-start | bytes 3833864 | tf_op jit(solution)/shard_map/ppermute | solution.py:20
  72.6 11.4 %copy-start.3 = (bf16[624,768]{1,0:T(8,128)(2,1)S(1)}, bf16[624,768]{1,0:T(8,128)(2,1)}, u32[]{:S(2)}) copy-start(bf16[624,768]{1,0:T(8,128)(2,1)} %copy-done.2) | copy-start | bytes 2875396
  74.7 55.3 %collective-permute-start.9 = (bf16[2,1,208,768]{3,2,1,0:T(8,128)(2,1)}, bf16[2,1,208,768]{3,2,1,0:T(8,128)(2,1)}, u32[]{:S(2)}, u32[]{:S(2)}) collective-permute-start(bf16[2,1,208,768]{3,2,1,0:T(8,128)(2,1)} %slice.37), channel_id=1, source_target_pairs={{0,2},{1,3},{4,6},{5,7},{8,10},{9,11},{12,14},{13,15},{16,18},{17,... | collective-permute-start | bytes 1916936 | tf_op jit(solution)/shard_map/ppermute | solution.py:20
  81.9 48.2 %collective-permute-start.6 = (bf16[2,1,208,768]{3,2,1,0:T(8,128)(2,1)}, bf16[2,1,208,768]{3,2,1,0:T(8,128)(2,1)}, u32[]{:S(2)}, u32[]{:S(2)}) collective-permute-start(bf16[2,1,208,768]{3,2,1,0:T(8,128)(2,1)} %slice.36), channel_id=1, source_target_pairs={{0,2},{1,3},{4,6},{5,7},{8,10},{9,11},{12,14},{13,15},{16,18},{17,... | collective-permute-start | bytes 1916936 | tf_op jit(solution)/shard_map/ppermute | solution.py:20
  159.7 2.7 %collective-permute-start.10 = (bf16[624,768]{1,0:T(8,128)(2,1)}, bf16[624,768]{1,0:T(8,128)(2,1)S(1)}, u32[]{:S(2)}, u32[]{:S(2)}) collective-permute-start(bf16[624,768]{1,0:T(8,128)(2,1)} %shard_map.119), channel_id=1, source_target_pairs={{0,1},{1,0},{2,3},{3,2},{4,5},{5,4},{6,7},{7,6},{8,9},{9,8},{10,11... | collective-permute-start | bytes 2875400 | tf_op jit(solution)/shard_map/ppermute | solution.py:57
  159.7 4.8 %copy-start.1 = (bf16[624,768]{1,0:T(8,128)(2,1)S(1)}, bf16[624,768]{1,0:T(8,128)(2,1)}, u32[]{:S(2)}) copy-start(bf16[624,768]{1,0:T(8,128)(2,1)} %reshape.51) | copy-start | bytes 2875396
  159.7 4.9 %copy-start.6 = (bf16[624,768]{1,0:T(8,128)(2,1)S(1)}, bf16[624,768]{1,0:T(8,128)(2,1)}, u32[]{:S(2)}) copy-start(bf16[624,768]{1,0:T(8,128)(2,1)} %shard_map.119) | copy-start | bytes 2875396
  (2 other events, 3.4 us)
